TPU v7x, 256 devices: a whole 4x4x8 slice. The times are simulated.
256 devices in a mesh: seq: 128 (over y_hi, x, z, core), tp: 2 (over y_lo).
Axes of the slice: x: 4, y: 4 (y_hi: 2, y_lo: 2; y = y_hi * 2 + y_lo), z: 8, core: 2. Of those that a mesh axis runs over, the one named last changes fastest.
Arguments:
- noisy: bfloat16 [2, 49152, 1024], P(None, 'seq', 'tp'), may hold values from -6 to 6
- levels: int32 [2], replicated, may hold values from 0 to 999, as said below
- pairs: int32 [384, 4], P('seq'), may hold values from 0 to 383, as said below
- w_qkv: bfloat16 [3, 1024, 1024], P(None, None, 'tp'), may hold values from -4 to 4
- w_out: bfloat16 [1024, 1024], P('tp'), may hold values from -0.1875 to 0.1875
- w_up: bfloat16 [1024, 3072], P(None, 'tp'), may hold values from -0.1875 to 0.1875
- w_down: bfloat16 [3072, 1024], P('tp'), may hold values from -0.109375 to 0.109375
Outputs:
- denoised: bfloat16 [2, 49152, 1024], P(None, 'seq', 'tp')
Inputs may be any that keep to these rules, and one draw needn't show every extreme that they name: For query block b and section s, pairs[b, s] lies in the group of 3 consecutive blocks numbered g XOR (384 * 128 // (384 * 2 ** (s + 1))), where g = b // 3; at each section the query blocks of one group name each block of that group once. The samples' levels differ from one another; one sample has level 999.
All inputs are finite; a program needn't handle non-finite values.
Results may differ from a plain program's by a relative error of at most 0.017.
Values may be sent and summed in bfloat16 or wider, within the bound.
No kernel may reach another device: no remote copies, remote signals or barrier semaphores. Data moves between devices by JAX's collectives and lax.ppermute only.
A program may use at most 192 MiB of HBM per device.

v0:
```python
import functools
import math

import jax
import jax.numpy as jnp
from jax import lax
from jax.experimental import pallas as pl
from jax.experimental.pallas import tpu as pltpu
from jax.sharding import PartitionSpec as P


D = 1024
HEADS = 16
BLOCK = 128
SECTIONS = 4


def partner(x, axis, stride):
    return lax.ppermute(x, axis, [(i, i ^ 1 << stride) for i in range(lax.axis_size(axis))])


def tp_swap(x):
    return lax.ppermute(x, "tp", [(0, 1), (1, 0)])


def other_w_out(w_out):
    seq_size = lax.axis_size("seq")
    tp_size = lax.axis_size("tp")
    far = seq_size // 2
    perm = [
        (s * tp_size + t, (s ^ far) * tp_size + (tp_size - 1 - t))
        for s in range(seq_size)
        for t in range(tp_size)
    ]
    return lax.ppermute(w_out, ("seq", "tp"), perm)


def tp_join(own, other, tp_index):
    first = jnp.where(tp_index == 0, own, other)
    second = jnp.where(tp_index == 0, other, own)
    return jnp.concatenate([first, second], axis=-1)


def tp_half(x, index, width):
    return lax.dynamic_slice_in_dim(x, index * width, width, axis=x.ndim - 1)


def near_kernel(q_ref, kn_ref, vn_ref, o_ref, m_ref, l_ref, *, head_dim):
    scale = 1.0 / math.sqrt(head_dim)
    dims = (((1,), (1,)), ((), ()))
    q = q_ref[0]
    key_near = kn_ref[0, 0]
    value_near = vn_ref[0, 0]
    first = lax.broadcasted_iota(jnp.int32, q.shape, 1) < head_dim
    parts = []
    for own in (first, jnp.logical_not(first)):
        q_head = jnp.where(own, q, jnp.zeros_like(q))
        scores = lax.dot_general(q_head, key_near, dims, preferred_element_type=jnp.float32) * scale
        top = scores.max(axis=-1, keepdims=True)
        expd = jnp.exp(scores - top)
        total = expd.sum(axis=-1, keepdims=True)
        mixed = jnp.dot(expd.astype(jnp.bfloat16), value_near, preferred_element_type=jnp.float32)
        parts.append((mixed, top, total))
    o_ref[0] = jnp.where(first, parts[0][0], parts[1][0])
    m_ref[0] = jnp.where(first, parts[0][1], parts[1][1])
    l_ref[0] = jnp.where(first, parts[0][2], parts[1][2])


def far_kernel(off_ref, q_ref, on_ref, mn_ref, ln_ref, *refs, head_dim):
    far_k = refs[0:2 * SECTIONS:2]
    far_v = refs[1:2 * SECTIONS:2]
    out_ref = refs[2 * SECTIONS]
    scale = 1.0 / math.sqrt(head_dim)
    dims = (((1,), (1,)), ((), ()))
    q = q_ref[0]
    tok_rows = q.shape[0]
    first = lax.broadcasted_iota(jnp.int32, q.shape, 1) < head_dim
    far_keys = []
    far_values = []
    for b in range(tok_rows // BLOCK):
        picks = [off_ref[b * SECTIONS + c] for c in range(SECTIONS)]
        far_keys.append(jnp.concatenate([far_k[c][0, 0, picks[c]] for c in range(SECTIONS)], axis=0))
        far_values.append(jnp.concatenate([far_v[c][0, 0, picks[c]] for c in range(SECTIONS)], axis=0))
    parts = []
    for own in (first, jnp.logical_not(first)):
        q_head = jnp.where(own, q, jnp.zeros_like(q))
        mixed, tops, totals = [], [], []
        for b in range(tok_rows // BLOCK):
            rows = slice(b * BLOCK, (b + 1) * BLOCK)
            scores = lax.dot_general(
                q_head[rows], far_keys[b], dims, preferred_element_type=jnp.float32
            ) * scale
            top = scores.max(axis=-1, keepdims=True)
            expd = jnp.exp(scores - top)
            totals.append(expd.sum(axis=-1, keepdims=True))
            tops.append(top)
            mixed.append(
                jnp.dot(expd.astype(jnp.bfloat16), far_values[b], preferred_element_type=jnp.float32)
            )
        parts.append(
            (
                jnp.concatenate(mixed, axis=0),
                jnp.concatenate(tops, axis=0),
                jnp.concatenate(totals, axis=0),
            )
        )
    far_o = jnp.where(first, parts[0][0], parts[1][0])
    far_m = jnp.where(first, parts[0][1], parts[1][1])
    far_l = jnp.where(first, parts[0][2], parts[1][2])
    near_o = on_ref[0]
    near_m = mn_ref[0]
    near_l = ln_ref[0]
    top = jnp.maximum(near_m, far_m)
    near_w = jnp.exp(near_m - top)
    far_w = jnp.exp(far_m - top)
    mixed = (near_o * near_w + far_o * far_w) / (near_l * near_w + far_l * far_w)
    out_ref[0] = mixed.astype(out_ref.dtype)


def near_attention(queries, kv_here, head_dim):
    _, tok_rows, width = queries.shape
    lanes = 2 * head_dim
    row_spec = pl.BlockSpec((1, tok_rows, lanes), lambda j: (0, 0, j))
    stat = jax.ShapeDtypeStruct(queries.shape, jnp.float32)
    return pl.pallas_call(
        functools.partial(near_kernel, head_dim=head_dim),
        grid=(width // lanes,),
        in_specs=[
            row_spec,
            pl.BlockSpec((1, 1, tok_rows, lanes), lambda j: (0, 0, 0, j)),
            pl.BlockSpec((1, 1, tok_rows, lanes), lambda j: (1, 0, 0, j)),
        ],
        out_specs=[row_spec, row_spec, row_spec],
        out_shape=[stat, stat, stat],
    )(queries, kv_here, kv_here)


def far_attention(queries, near, got, offsets, head_dim):
    _, tok_rows, width = queries.shape
    blocks_dev = tok_rows // BLOCK
    lanes = 2 * head_dim
    row_spec = pl.BlockSpec((1, tok_rows, lanes), lambda j, off: (0, 0, j))
    in_specs = [row_spec, row_spec, row_spec, row_spec]
    operands = [queries, *near]
    for section_idx in range(SECTIONS):
        for which in range(2):
            in_specs.append(
                pl.BlockSpec(
                    (1, 1, blocks_dev, BLOCK, lanes),
                    lambda j, off, w=which: (w, 0, 0, 0, j),
                )
            )
            operands.append(got[section_idx])
    grid_spec = pltpu.PrefetchScalarGridSpec(
        num_scalar_prefetch=1,
        grid=(width // lanes,),
        in_specs=in_specs,
        out_specs=row_spec,
    )
    return pl.pallas_call(
        functools.partial(far_kernel, head_dim=head_dim),
        grid_spec=grid_spec,
        out_shape=jax.ShapeDtypeStruct(queries.shape, queries.dtype),
    )(offsets, *operands)


def level_features(levels, model_width):
    half_count = model_width // 2
    index_row = jnp.arange(half_count, dtype=jnp.float32)
    freqs = jnp.exp(-math.log(10000.0) * index_row / half_count)
    angles = levels.astype(jnp.float32)[:, None] * freqs[None, :]
    return jnp.concatenate([jnp.sin(angles), jnp.cos(angles)], axis=1)


def rms_norm(values):
    return values * lax.rsqrt(jnp.mean(values * values, axis=-1, keepdims=True) + 1e-06)


def condition(gathered, level_feat):
    return (rms_norm(gathered.astype(jnp.float32)) + level_feat[:, None, :]).astype(jnp.bfloat16)


def per_device(noisy, levels, pairs, w_qkv, w_out, w_up, w_down):
    level_feat = level_features(levels, D)
    w_out_other = other_w_out(w_out)
    outs = []
    for s in range(noisy.shape[0]):
        outs.append(
            one_sample(
                noisy[s:s + 1], level_feat[s:s + 1], pairs, w_qkv, w_out, w_out_other,
                w_up, w_down,
            )
        )
    return jnp.concatenate(outs, axis=0)


def one_sample(noisy, level_feat, pairs, w_qkv, w_out, w_out_other, w_up, w_down):
    samples, tok_rows, half_width = noisy.shape
    tp_index = lax.axis_index("tp")
    noisy_other = tp_swap(noisy)
    gathered = tp_join(noisy, noisy_other, tp_index)
    normed = condition(gathered, level_feat)
    projected = jnp.einsum(
        "std,cde->cste", normed, w_qkv, preferred_element_type=jnp.float32
    ).astype(jnp.bfloat16)
    queries, keys_here, values_here = (projected[0], projected[1], projected[2])
    blocks_dev = tok_rows // BLOCK
    head_dim = D // HEADS
    local_width = w_qkv.shape[2]
    axis_bits = lax.axis_size("seq").bit_length() - 1
    kv_here = jnp.stack([keys_here, values_here])
    offsets = (pairs % blocks_dev).astype(jnp.int32).reshape(-1)
    got = [None] * SECTIONS
    for section_idx in reversed(range(SECTIONS)):
        bit_pos = axis_bits - 1 - section_idx
        got[section_idx] = partner(kv_here, "seq", bit_pos).reshape(
            2, samples, blocks_dev, BLOCK, local_width
        )
    near = near_attention(queries, kv_here, head_dim)
    mixed = far_attention(queries, near, got, offsets, head_dim)
    mixed_other = tp_swap(mixed)
    attn = jnp.einsum("sth,hd->std", mixed, w_out, preferred_element_type=jnp.float32)
    attn = attn + jnp.einsum(
        "sth,hd->std", mixed_other, w_out_other, preferred_element_type=jnp.float32
    )
    middle = (gathered.astype(jnp.float32) + attn).astype(jnp.bfloat16)
    middle_half = tp_half(middle, tp_index, half_width)
    inner = rms_norm(middle.astype(jnp.float32)).astype(jnp.bfloat16)
    hidden = jax.nn.gelu(
        jnp.einsum("std,df->stf", inner, w_up, preferred_element_type=jnp.float32), approximate=True
    ).astype(jnp.bfloat16)
    down_part = jnp.einsum("stf,fd->std", hidden, w_down, preferred_element_type=jnp.float32)
    down_own = tp_half(down_part, tp_index, half_width)
    down_send = tp_half(down_part, 1 - tp_index, half_width).astype(jnp.bfloat16)
    down_half = down_own + tp_swap(down_send).astype(jnp.float32)
    return (middle_half.astype(jnp.float32) + down_half).astype(jnp.bfloat16)


def solution(mesh):
    in_specs = (
        P(None, "seq", "tp"),
        P(),
        P("seq", None),
        P(None, None, "tp"),
        P("tp", None),
        P(None, "tp"),
        P("tp", None),
    )
    out_specs = P(None, "seq", "tp")
    return jax.shard_map(
        per_device, mesh=mesh, in_specs=in_specs, out_specs=out_specs, check_vma=False
    )
```

profile of v0, /device:TPU:36, one launch (start us, length us, event | category | flops | bytes accessed | tf_op | source)
XLA Modules:
  0.0 173.9 jit_solution(16071118659870816063)
XLA Ops:
  3.7 8.5 %collective-permute-done = bf16[1,384,512]{2,1,0:T(8,128)(2,1)} collective-permute-done((bf16[1,384,512]{2,1,0:T(8,128)(2,1)S(1)}, bf16[1,384,512]{2,1,0:T(8,128)(2,1)}, u32[]{:S(2)}, u32[]{:S(2)}) %collective-permute-start) | collective-permute-done | bytes 393248 | tf_op jit(solution)/shard_map/ppermute | solution.py:23
  12.2 2.1 %broadcast_select_fusion.3 = (bf16[1,384,512]{2,1,0:T(8,128)(2,1)S(1)}, bf16[1,384,512]{2,1,0:T(8,128)(2,1)S(1)}, bf16[1,384,512]{2,1,0:T(8,128)(2,1)}) fusion(bf16[1,384,512]{2,1,0:T(8,128)(2,1)} %collective-permute-done, pred[]{:T(512)S(6)} %eq.5, bf16[2,384,512]{2,1,0:T(8,128)(2,1)} %param.7), kind=kLoop, calls=%fused_computation.86 | loop fusion | flops 393216 | bytes 2359297 | tf_op jit(solution)/shard_map/jit(_where)/select_n | solution.py:39
  17.3 3.2 %collective-permute-start.1 = (bf16[2,1,384,512]{3,2,1,0:T(8,128)(2,1)}, bf16[2,1,384,512]{3,2,1,0:T(8,128)(2,1)}, u32[]{:S(2)}, u32[]{:S(2)}) collective-permute-start(bf16[2,1,384,512]{3,2,1,0:T(8,128)(2,1)} %stack.8.kn_ref.vn_ref), channel_id=1, source_target_pairs={{0,128},{2,130},{4,132},{6,134},{8,136},{10,138},{12,140},{14,142}... | collective-permute-start | bytes 2359304 | tf_op jit(solution)/shard_map/ppermute | solution.py:19
  21.0 2.1 %collective-permute-start.3 = (bf16[2,1,384,512]{3,2,1,0:T(8,128)(2,1)}, bf16[2,1,384,512]{3,2,1,0:T(8,128)(2,1)}, u32[]{:S(2)}, u32[]{:S(2)}) collective-permute-start(bf16[2,1,384,512]{3,2,1,0:T(8,128)(2,1)} %stack.8.kn_ref.vn_ref), channel_id=1, source_target_pairs={{0,32},{2,34},{4,36},{6,38},{8,40},{10,42},{12,44},{14,46},{16,48}... | collective-permute-start | bytes 2359304 | tf_op jit(solution)/shard_map/ppermute | solution.py:19
  23.1 6.3 %collective-permute-start.4 = (bf16[2,1,384,512]{3,2,1,0:T(8,128)(2,1)}, bf16[2,1,384,512]{3,2,1,0:T(8,128)(2,1)}, u32[]{:S(2)}, u32[]{:S(2)}) collective-permute-start(bf16[2,1,384,512]{3,2,1,0:T(8,128)(2,1)} %stack.8.kn_ref.vn_ref), channel_id=1, source_target_pairs={{0,16},{2,18},{4,20},{6,22},{8,24},{10,26},{12,28},{14,30},{16,0},... | collective-permute-start | bytes 2359304 | tf_op jit(solution)/shard_map/ppermute | solution.py:19
  32.4 5.4 %shard_map.73 = (f32[1,384,512]{2,1,0:T(8,128)}, f32[1,384,512]{2,1,0:T(8,128)}, f32[1,384,512]{2,1,0:T(8,128)}) custom-call(bf16[1,384,512]{2,1,0:T(8,128)(2,1)} %slice_bitcast_fusion.1.q_ref, bf16[2,1,384,512]{3,2,1,0:T(8,128)(2,1)} %stack.8.kn_ref.vn_ref, bf16[2,1,384,512]{3,2,1,0:T(8,128)(2,1)} %stack.8.kn_ref.vn_ref), custom_call_target="tpu_custom_call" | custom-call | tf_op jit(solution)/shard_map/pallas_call | solution.py:125
  37.9 8.4 %collective-permute-done.8 = bf16[1,384,512]{2,1,0:T(8,128)(2,1)} collective-permute-done((bf16[1,384,512]{2,1,0:T(8,128)(2,1)}, bf16[1,384,512]{2,1,0:T(8,128)(2,1)}, u32[]{:S(2)}, u32[]{:S(2)}) %collective-permute-start.8) | collective-permute-done | bytes 393248 | tf_op jit(solution)/shard_map/ppermute | solution.py:23
  48.7 7.7 %collective-permute-done.3 = bf16[2,1,384,512]{3,2,1,0:T(8,128)(2,1)} collective-permute-done((bf16[2,1,384,512]{3,2,1,0:T(8,128)(2,1)}, bf16[2,1,384,512]{3,2,1,0:T(8,128)(2,1)}, u32[]{:S(2)}, u32[]{:S(2)}) %collective-permute-start.3) | collective-permute-done | bytes 786464 | tf_op jit(solution)/shard_map/ppermute | solution.py:19
  56.4 6.2 %collective-permute-done.4 = bf16[2,1,384,512]{3,2,1,0:T(8,128)(2,1)} collective-permute-done((bf16[2,1,384,512]{3,2,1,0:T(8,128)(2,1)}, bf16[2,1,384,512]{3,2,1,0:T(8,128)(2,1)}, u32[]{:S(2)}, u32[]{:S(2)}) %collective-permute-start.4) | collective-permute-done | bytes 786464 | tf_op jit(solution)/shard_map/ppermute | solution.py:19
  62.6 12.4 %shard_map.74 = bf16[1,384,512]{2,1,0:T(8,128)(2,1)} custom-call(s32[12]{0:T(128)} %reshape.290.off_ref, bf16[1,384,512]{2,1,0:T(8,128)(2,1)} %slice_bitcast_fusion.1.q_ref, f32[1,384,512]{2,1,0:T(8,128)} %get-tuple-element.11.on_ref, f32[1,384,512]{2,1,0:T(8,128)} %get-tuple-element.12.mn_ref, f32[1,384,512]{2,1,0:T(8,128)} %get-tuple-element.13.ln_ref, ...), custom_call_target="tpu_custom_call" | custom-call | tf_op jit(solution)/shard_map/pallas_call | solution.py:160
  75.7 2.6 %fusion.27 = bf16[3,1,384,512]{3,2,1,0:T(8,128)(2,1)S(1)} fusion(bf16[3,1024,512]{2,1,0:T(8,128)(2,1)S(1)} %copy-done, f32[1024]{0:T(1024)S(1)} %bitcast.88, f32[384]{0:T(512)S(1)} %add_rsqrt_fusion.1, bf16[384,512]{1,0:T(8,128)(2,1)} %bitcast.86, bf16[384,512]{1,0:T(8,128)(2,1)} %bitcast.84), kind=kOutput, calls=%fused_computation.41 | convolution fusion | flops 1211301888 | bytes 5117440 | tf_op jit(solution)/shard_map/std,cde->cste/dot_general | solution.py:203
  82.6 2.0 %collective-permute-start.11 = (bf16[2,1,384,512]{3,2,1,0:T(8,128)(2,1)}, bf16[2,1,384,512]{3,2,1,0:T(8,128)(2,1)}, u32[]{:S(2)}, u32[]{:S(2)}) collective-permute-start(bf16[2,1,384,512]{3,2,1,0:T(8,128)(2,1)} %stack.9.kn_ref.vn_ref), channel_id=1, source_target_pairs={{0,32},{2,34},{4,36},{6,38},{8,40},{10,42},{12,44},{14,46},{16,48}... | collective-permute-start | bytes 2359304 | tf_op jit(solution)/shard_map/ppermute | solution.py:19
  85.4 5.4 %shard_map.75 = (f32[1,384,512]{2,1,0:T(8,128)}, f32[1,384,512]{2,1,0:T(8,128)}, f32[1,384,512]{2,1,0:T(8,128)}) custom-call(bf16[1,384,512]{2,1,0:T(8,128)(2,1)} %slice_bitcast_fusion.q_ref, bf16[2,1,384,512]{3,2,1,0:T(8,128)(2,1)} %stack.9.kn_ref.vn_ref, bf16[2,1,384,512]{3,2,1,0:T(8,128)(2,1)} %stack.9.kn_ref.vn_ref), custom_call_target="tpu_custom_call" | custom-call | tf_op jit(solution)/shard_map/pallas_call | solution.py:125
  90.9 5.5 %collective-permute-start.12 = (bf16[2,1,384,512]{3,2,1,0:T(8,128)(2,1)}, bf16[2,1,384,512]{3,2,1,0:T(8,128)(2,1)}, u32[]{:S(2)}, u32[]{:S(2)}) collective-permute-start(bf16[2,1,384,512]{3,2,1,0:T(8,128)(2,1)} %stack.9.kn_ref.vn_ref), channel_id=1, source_target_pairs={{0,16},{2,18},{4,20},{6,22},{8,24},{10,26},{12,28},{14,30},{16,0},... | collective-permute-start | bytes 2359304 | tf_op jit(solution)/shard_map/ppermute | solution.py:19
  96.4 1.9 %fusion.71 = f32[384,1024]{1,0:T(8,128)S(1)} fusion(bf16[512,1024]{1,0:T(8,128)(2,1)} %collective-permute-done.6, bf16[1,384,512]{2,1,0:T(8,128)(2,1)} %collective-permute-done.5), kind=kOutput, calls=%fused_computation.80 | convolution fusion | flops 402653184 | bytes 3014656 | tf_op jit(solution)/shard_map/sth,hd->std/dot_general | solution.py:223
  103.3 13.2 %collective-permute-done.11 = bf16[2,1,384,512]{3,2,1,0:T(8,128)(2,1)} collective-permute-done((bf16[2,1,384,512]{3,2,1,0:T(8,128)(2,1)}, bf16[2,1,384,512]{3,2,1,0:T(8,128)(2,1)}, u32[]{:S(2)}, u32[]{:S(2)}) %collective-permute-start.11) | collective-permute-done | bytes 786464 | tf_op jit(solution)/shard_map/ppermute | solution.py:19
  116.5 8.2 %collective-permute-done.12 = bf16[2,1,384,512]{3,2,1,0:T(8,128)(2,1)} collective-permute-done((bf16[2,1,384,512]{3,2,1,0:T(8,128)(2,1)}, bf16[2,1,384,512]{3,2,1,0:T(8,128)(2,1)}, u32[]{:S(2)}, u32[]{:S(2)}) %collective-permute-start.12) | collective-permute-done | bytes 786464 | tf_op jit(solution)/shard_map/ppermute | solution.py:19
  124.7 12.4 %shard_map.76 = bf16[1,384,512]{2,1,0:T(8,128)(2,1)} custom-call(s32[12]{0:T(128)} %reshape.290.off_ref, bf16[1,384,512]{2,1,0:T(8,128)(2,1)} %slice_bitcast_fusion.q_ref, f32[1,384,512]{2,1,0:T(8,128)} %get-tuple-element.14.on_ref, f32[1,384,512]{2,1,0:T(8,128)} %get-tuple-element.15.mn_ref, f32[1,384,512]{2,1,0:T(8,128)} %get-tuple-element.16.ln_ref, ...), custom_call_target="tpu_custom_call" | custom-call | tf_op jit(solution)/shard_map/pallas_call | solution.py:160
  137.2 7.0 %fusion.30 = f32[384,1024]{1,0:T(8,128)} fusion(bf16[1536,1024]{1,0:T(8,128)(2,1)} %param.13, bf16[1024,1536]{1,0:T(8,128)(2,1)} %param.12, bf16[384,1024]{1,0:T(8,128)(2,1)} %get-tuple-element.29, f32[384]{0:T(512)S(1)} %add_rsqrt_fusion.2), kind=kOutput, calls=%fused_computation.43 | convolution fusion | flops 2422407168 | bytes 8652288 | tf_op jit(solution)/shard_map/stf,fd->std/dot_general | solution.py:232
  144.2 1.9 %fusion.66 = bf16[1,384,512]{2,1,0:T(8,128)(2,1)} fusion(f32[384,1024]{1,0:T(8,128)} %fusion.30, s32[]{:T(128)S(6)} %select_n.44), kind=kLoop, calls=%fused_computation.73 | loop fusion | bytes 786436 | tf_op jit(solution)/shard_map/convert_element_type | solution.py:234
  146.2 2.1 %collective-permute-start.7 = (bf16[1,384,512]{2,1,0:T(8,128)(2,1)}, bf16[1,384,512]{2,1,0:T(8,128)(2,1)S(1)}, u32[]{:S(2)}, u32[]{:S(2)}) collective-permute-start(bf16[1,384,512]{2,1,0:T(8,128)(2,1)} %fusion.66), channel_id=1, source_target_pairs={{0,1},{1,0},{2,3},{3,2},{4,5},{5,4},{6,7},{7,6},{8,9},{9,8},{10,11... | collective-permute-start | bytes 1179656 | tf_op jit(solution)/shard_map/ppermute | solution.py:23
  152.1 7.0 %fusion.28 = f32[384,1024]{1,0:T(8,128)} fusion(bf16[1536,1024]{1,0:T(8,128)(2,1)} %param.13, bf16[1024,1536]{1,0:T(8,128)(2,1)} %param.12, bf16[384,1024]{1,0:T(8,128)(2,1)} %get-tuple-element.27, f32[384]{0:T(512)S(1)} %add_rsqrt_fusion), kind=kOutput, calls=%fused_computation.42 | convolution fusion | flops 2422407168 | bytes 8652288 | tf_op jit(solution)/shard_map/stf,fd->std/dot_general | solution.py:232
  159.1 2.0 %fusion.67 = bf16[1,384,512]{2,1,0:T(8,128)(2,1)} fusion(f32[384,1024]{1,0:T(8,128)} %fusion.28, s32[]{:T(128)S(6)} %select_n.44), kind=kLoop, calls=%fused_computation.74 | loop fusion | bytes 786436 | tf_op jit(solution)/shard_map/convert_element_type | solution.py:234
  162.9 8.7 %collective-permute-done.14 = bf16[1,384,512]{2,1,0:T(8,128)(2,1)} collective-permute-done((bf16[1,384,512]{2,1,0:T(8,128)(2,1)}, bf16[1,384,512]{2,1,0:T(8,128)(2,1)}, u32[]{:S(2)}, u32[]{:S(2)}) %collective-permute-start.14) | collective-permute-done | bytes 393248 | tf_op jit(solution)/shard_map/ppermute | solution.py:23
  (70 shorter events, 31.3 us)
Async XLA Ops:
  0.0 14.5 %copy-start = (bf16[3,1024,512]{2,1,0:T(8,128)(2,1)S(1)}, bf16[3,1024,512]{2,1,0:T(8,128)(2,1)}, u32[]{:S(2)}) copy-start(bf16[3,1024,512]{2,1,0:T(8,128)(2,1)} %param.10) | copy-start | bytes 9437188
  1.2 11.0 %collective-permute-start = (bf16[1,384,512]{2,1,0:T(8,128)(2,1)S(1)}, bf16[1,384,512]{2,1,0:T(8,128)(2,1)}, u32[]{:S(2)}, u32[]{:S(2)}) collective-permute-start(bf16[1,384,512]{2,1,0:T(8,128)(2,1)S(1)} %slice.28), channel_id=1, source_target_pairs={{0,1},{1,0},{2,3},{3,2},{4,5},{5,4},{6,7},{7,6},{8,9},{9,8},{10,11... | collective-permute-start | bytes 1179656 | tf_op jit(solution)/shard_map/ppermute | solution.py:23
  16.0 14.0 %copy-start.11 = (s32[3,4]{1,0:T(4,128)S(1)}, s32[3,4]{1,0:T(4,128)}, u32[]{:S(2)}) copy-start(s32[3,4]{1,0:T(4,128)} %param.9) | copy-start | bytes 148
  17.3 31.4 %collective-permute-start.1 = (bf16[2,1,384,512]{3,2,1,0:T(8,128)(2,1)}, bf16[2,1,384,512]{3,2,1,0:T(8,128)(2,1)}, u32[]{:S(2)}, u32[]{:S(2)}) collective-permute-start(bf16[2,1,384,512]{3,2,1,0:T(8,128)(2,1)} %stack.8.kn_ref.vn_ref), channel_id=1, source_target_pairs={{0,128},{2,130},{4,132},{6,134},{8,136},{10,138},{12,140},{14,142}... | collective-permute-start | bytes 2359304 | tf_op jit(solution)/shard_map/ppermute | solution.py:19
  20.5 28.2 %collective-permute-start.2 = (bf16[2,1,384,512]{3,2,1,0:T(8,128)(2,1)}, bf16[2,1,384,512]{3,2,1,0:T(8,128)(2,1)}, u32[]{:S(2)}, u32[]{:S(2)}) collective-permute-start(bf16[2,1,384,512]{3,2,1,0:T(8,128)(2,1)} %stack.8.kn_ref.vn_ref), channel_id=1, source_target_pairs={{0,64},{2,66},{4,68},{6,70},{8,72},{10,74},{12,76},{14,78},{16,80}... | collective-permute-start | bytes 2359304 | tf_op jit(solution)/shard_map/ppermute | solution.py:19
  21.0 35.4 %collective-permute-start.3 = (bf16[2,1,384,512]{3,2,1,0:T(8,128)(2,1)}, bf16[2,1,384,512]{3,2,1,0:T(8,128)(2,1)}, u32[]{:S(2)}, u32[]{:S(2)}) collective-permute-start(bf16[2,1,384,512]{3,2,1,0:T(8,128)(2,1)} %stack.8.kn_ref.vn_ref), channel_id=1, source_target_pairs={{0,32},{2,34},{4,36},{6,38},{8,40},{10,42},{12,44},{14,46},{16,48}... | collective-permute-start | bytes 2359304 | tf_op jit(solution)/shard_map/ppermute | solution.py:19
  23.1 39.5 %collective-permute-start.4 = (bf16[2,1,384,512]{3,2,1,0:T(8,128)(2,1)}, bf16[2,1,384,512]{3,2,1,0:T(8,128)(2,1)}, u32[]{:S(2)}, u32[]{:S(2)}) collective-permute-start(bf16[2,1,384,512]{3,2,1,0:T(8,128)(2,1)} %stack.8.kn_ref.vn_ref), channel_id=1, source_target_pairs={{0,16},{2,18},{4,20},{6,22},{8,24},{10,26},{12,28},{14,30},{16,0},... | collective-permute-start | bytes 2359304 | tf_op jit(solution)/shard_map/ppermute | solution.py:19
  29.4 16.9 %collective-permute-start.8 = (bf16[1,384,512]{2,1,0:T(8,128)(2,1)}, bf16[1,384,512]{2,1,0:T(8,128)(2,1)}, u32[]{:S(2)}, u32[]{:S(2)}) collective-permute-start(bf16[1,384,512]{2,1,0:T(8,128)(2,1)} %get-tuple-element.21), channel_id=1, source_target_pairs={{0,1},{1,0},{2,3},{3,2},{4,5},{5,4},{6,7},{7,6},{8,9},{9,8},{10,11... | collective-permute-start | bytes 1179656 | tf_op jit(solution)/shard_map/ppermute | solution.py:23
  46.3 44.6 %collective-permute-start.6 = (bf16[512,1024]{1,0:T(8,128)(2,1)}, bf16[512,1024]{1,0:T(8,128)(2,1)}, u32[]{:S(2)}, u32[]{:S(2)}) collective-permute-start(bf16[512,1024]{1,0:T(8,128)(2,1)} %param.11), channel_id=1, source_target_pairs={{0,129},{1,128},{2,131},{3,130},{4,133},{5,132},{6,135},{7,134},{8... | collective-permute-start | bytes 3145736 | tf_op jit(solution)/shard_map/ppermute | solution.py:35
  75.0 21.5 %collective-permute-start.5 = (bf16[1,384,512]{2,1,0:T(8,128)(2,1)}, bf16[1,384,512]{2,1,0:T(8,128)(2,1)}, u32[]{:S(2)}, u32[]{:S(2)}) collective-permute-start(bf16[1,384,512]{2,1,0:T(8,128)(2,1)} %shard_map.74), channel_id=1, source_target_pairs={{0,1},{1,0},{2,3},{3,2},{4,5},{5,4},{6,7},{7,6},{8,9},{9,8},{10,11... | collective-permute-start | bytes 1179656 | tf_op jit(solution)/shard_map/ppermute | solution.py:23
  79.2 22.3 %collective-permute-start.9 = (bf16[2,1,384,512]{3,2,1,0:T(8,128)(2,1)}, bf16[2,1,384,512]{3,2,1,0:T(8,128)(2,1)}, u32[]{:S(2)}, u32[]{:S(2)}) collective-permute-start(bf16[2,1,384,512]{3,2,1,0:T(8,128)(2,1)} %stack.9.kn_ref.vn_ref), channel_id=1, source_target_pairs={{0,128},{2,130},{4,132},{6,134},{8,136},{10,138},{12,140},{14,142}... | collective-permute-start | bytes 2359304 | tf_op jit(solution)/shard_map/ppermute | solution.py:19
  81.1 22.2 %collective-permute-start.10 = (bf16[2,1,384,512]{3,2,1,0:T(8,128)(2,1)}, bf16[2,1,384,512]{3,2,1,0:T(8,128)(2,1)}, u32[]{:S(2)}, u32[]{:S(2)}) collective-permute-start(bf16[2,1,384,512]{3,2,1,0:T(8,128)(2,1)} %stack.9.kn_ref.vn_ref), channel_id=1, source_target_pairs={{0,64},{2,66},{4,68},{6,70},{8,72},{10,74},{12,76},{14,78},{16,80}... | collective-permute-start | bytes 2359304 | tf_op jit(solution)/shard_map/ppermute | solution.py:19
  82.6 33.9 %collective-permute-start.11 = (bf16[2,1,384,512]{3,2,1,0:T(8,128)(2,1)}, bf16[2,1,384,512]{3,2,1,0:T(8,128)(2,1)}, u32[]{:S(2)}, u32[]{:S(2)}) collective-permute-start(bf16[2,1,384,512]{3,2,1,0:T(8,128)(2,1)} %stack.9.kn_ref.vn_ref), channel_id=1, source_target_pairs={{0,32},{2,34},{4,36},{6,38},{8,40},{10,42},{12,44},{14,46},{16,48}... | collective-permute-start | bytes 2359304 | tf_op jit(solution)/shard_map/ppermute | solution.py:19
  90.8 7.5 %copy-start.2 = (bf16[1,384,512]{2,1,0:T(8,128)(2,1)S(1)}, bf16[1,384,512]{2,1,0:T(8,128)(2,1)}, u32[]{:S(2)}) copy-start(bf16[1,384,512]{2,1,0:T(8,128)(2,1)} %copy-done.1) | copy-start | bytes 1179652
  90.8 7.5 %copy-start.9 = (bf16[1,384,512]{2,1,0:T(8,128)(2,1)S(1)}, bf16[1,384,512]{2,1,0:T(8,128)(2,1)}, u32[]{:S(2)}) copy-start(bf16[1,384,512]{2,1,0:T(8,128)(2,1)} %shard_map.74) | copy-start | bytes 1179652
  90.8 7.5 %copy-start.12 = (bf16[512,1024]{1,0:T(8,128)(2,1)S(1)}, bf16[512,1024]{1,0:T(8,128)(2,1)}, u32[]{:S(2)}) copy-start(bf16[512,1024]{1,0:T(8,128)(2,1)} %param.11) | copy-start | bytes 3145732
  90.9 33.8 %collective-permute-start.12 = (bf16[2,1,384,512]{3,2,1,0:T(8,128)(2,1)}, bf16[2,1,384,512]{3,2,1,0:T(8,128)(2,1)}, u32[]{:S(2)}, u32[]{:S(2)}) collective-permute-start(bf16[2,1,384,512]{3,2,1,0:T(8,128)(2,1)} %stack.9.kn_ref.vn_ref), channel_id=1, source_target_pairs={{0,16},{2,18},{4,20},{6,22},{8,24},{10,26},{12,28},{14,30},{16,0},... | collective-permute-start | bytes 2359304 | tf_op jit(solution)/shard_map/ppermute | solution.py:19
  137.1 11.4 %collective-permute-start.13 = (bf16[1,384,512]{2,1,0:T(8,128)(2,1)}, bf16[1,384,512]{2,1,0:T(8,128)(2,1)}, u32[]{:S(2)}, u32[]{:S(2)}) collective-permute-start(bf16[1,384,512]{2,1,0:T(8,128)(2,1)} %shard_map.76), channel_id=1, source_target_pairs={{0,1},{1,0},{2,3},{3,2},{4,5},{5,4},{6,7},{7,6},{8,9},{9,8},{10,11... | collective-permute-start | bytes 1179656 | tf_op jit(solution)/shard_map/ppermute | solution.py:23
  146.2 4.3 %copy-start.6 = (bf16[1,384,512]{2,1,0:T(8,128)(2,1)S(1)}, bf16[1,384,512]{2,1,0:T(8,128)(2,1)}, u32[]{:S(2)}) copy-start(bf16[1,384,512]{2,1,0:T(8,128)(2,1)} %copy-done.5) | copy-start | bytes 1179652
  146.2 4.3 %copy-start.10 = (bf16[1,384,512]{2,1,0:T(8,128)(2,1)S(1)}, bf16[1,384,512]{2,1,0:T(8,128)(2,1)}, u32[]{:S(2)}) copy-start(bf16[1,384,512]{2,1,0:T(8,128)(2,1)} %shard_map.76) | copy-start | bytes 1179652
  146.2 4.3 %copy-start.13 = (bf16[512,1024]{1,0:T(8,128)(2,1)S(1)}, bf16[512,1024]{1,0:T(8,128)(2,1)}, u32[]{:S(2)}) copy-start(bf16[512,1024]{1,0:T(8,128)(2,1)} %param.11) | copy-start | bytes 3145732
  146.2 15.2 %collective-permute-start.7 = (bf16[1,384,512]{2,1,0:T(8,128)(2,1)}, bf16[1,384,512]{2,1,0:T(8,128)(2,1)S(1)}, u32[]{:S(2)}, u32[]{:S(2)}) collective-permute-start(bf16[1,384,512]{2,1,0:T(8,128)(2,1)} %fusion.66), channel_id=1, source_target_pairs={{0,1},{1,0},{2,3},{3,2},{4,5},{5,4},{6,7},{7,6},{8,9},{9,8},{10,11... | collective-permute-start | bytes 1179656 | tf_op jit(solution)/shard_map/ppermute | solution.py:23
  161.1 10.5 %collective-permute-start.14 = (bf16[1,384,512]{2,1,0:T(8,128)(2,1)}, bf16[1,384,512]{2,1,0:T(8,128)(2,1)}, u32[]{:S(2)}, u32[]{:S(2)}) collective-permute-start(bf16[1,384,512]{2,1,0:T(8,128)(2,1)} %fusion.67), channel_id=1, source_target_pairs={{0,1},{1,0},{2,3},{3,2},{4,5},{5,4},{6,7},{7,6},{8,9},{9,8},{10,11... | collective-permute-start | bytes 1179656 | tf_op jit(solution)/shard_map/ppermute | solution.py:23
  161.4 10.2 %copy-start.8 = (f32[384,1024]{1,0:T(8,128)S(1)}, f32[384,1024]{1,0:T(8,128)}, u32[]{:S(2)}) copy-start(f32[384,1024]{1,0:T(8,128)} %fusion.28) | copy-start | bytes 4718596
  (5 other events, 9.0 us)
where the time goes:
time: 175 us; the launch traced here: 174 us
  waiting for transfers between devices  64.6 us (37%)
  Pallas kernels  35.6 us (20%)
  starting transfers between devices  28.8 us (16%)
  matrix products  25.1 us (14%)
  local copies, waits for them, and re-layouts  11.2 us (6%)
  other arithmetic  8.3 us (5%)
    ppermute x8, waiting for transfers between devices, partner(): lax.ppermute(x, axis, [(i, i ^ 1 << stride) for i in range(lax.axis_size(...  38.6 us
    ppermute x6, waiting for transfers between devices, tp_swap(): return lax.ppermute(x, 'tp', [(0, 1), (1, 0)])  25.9 us
    pallas_call x2, Pallas kernels, far_attention(): pl.pallas_call(functools.partial(far_kernel, head_dim=head_dim), grid_spe...  24.8 us
    ppermute x8, starting transfers between devices, partner(): lax.ppermute(x, axis, [(i, i ^ 1 << stride) for i in range(lax.axis_size(...  23 us
    dot_general x2, matrix products, one_sample(): jnp.einsum('stf,fd->std', hidden, w_down, preferred_element_type=jnp.floa...  14.1 us
    pallas_call x2, Pallas kernels, near_attention(): pl.pallas_call(functools.partial(near_kernel, head_dim=head_dim), grid=(w...  10.8 us
    ppermute x6, starting transfers between devices, tp_swap(): return lax.ppermute(x, 'tp', [(0, 1), (1, 0)])  5.59 us
    dot_general x2, matrix products, one_sample(): jnp.einsum('std,cde->cste', normed, w_qkv, preferred_element_type=jnp.flo...  4.02 us
  transfers between devices with their start and end apart: 15, of which 10 were waited for; matrix products, arithmetic and copies ran while one was open for 20% of the time, Pallas kernels for 13%

commit v1 on v0

--- a/solution.py
+++ b/solution.py
@@ -183,6 +183,9 @@
 def per_device(noisy, levels, pairs, w_qkv, w_out, w_up, w_down):
     level_feat = level_features(levels, D)
     w_out_other = other_w_out(w_out)
+    tp_index = lax.axis_index("tp")
+    half_width = noisy.shape[2]
+    w_down = (tp_half(w_down, 1 - tp_index, half_width), tp_half(w_down, tp_index, half_width))
     outs = []
     for s in range(noisy.shape[0]):
         outs.append(
@@ -229,10 +232,13 @@
     hidden = jax.nn.gelu(
         jnp.einsum("std,df->stf", inner, w_up, preferred_element_type=jnp.float32), approximate=True
     ).astype(jnp.bfloat16)
-    down_part = jnp.einsum("stf,fd->std", hidden, w_down, preferred_element_type=jnp.float32)
-    down_own = tp_half(down_part, tp_index, half_width)
-    down_send = tp_half(down_part, 1 - tp_index, half_width).astype(jnp.bfloat16)
-    down_half = down_own + tp_swap(down_send).astype(jnp.float32)
+    w_down_send, w_down_own = w_down
+    down_send = jnp.einsum(
+        "stf,fd->std", hidden, w_down_send, preferred_element_type=jnp.float32
+    ).astype(jnp.bfloat16)
+    down_received = tp_swap(down_send)
+    down_own = jnp.einsum("stf,fd->std", hidden, w_down_own, preferred_element_type=jnp.float32)
+    down_half = down_own + down_received.astype(jnp.float32)
     return (middle_half.astype(jnp.float32) + down_half).astype(jnp.bfloat16)
 
 

time: 175 us -> 170 us (0.971)
  the two profiles are of different devices: /device:TPU:36 before, /device:TPU:34 now
where the time goes in v1:
time: 170 us; the launch traced here: 169 us
  waiting for transfers between devices  66.8 us (39%)
  Pallas kernels  35.6 us (21%)
  starting transfers between devices  28.5 us (17%)
  matrix products  23.6 us (14%)
  local copies, waits for them, and re-layouts  8.72 us (5%)
  other arithmetic  5.52 us (3%)
    ppermute x8, waiting for transfers between devices, partner(): lax.ppermute(x, axis, [(i, i ^ 1 << stride) for i in range(lax.axis_size(...  39.6 us
    ppermute x6, waiting for transfers between devices, tp_swap(): return lax.ppermute(x, 'tp', [(0, 1), (1, 0)])  27.2 us
    pallas_call x2, Pallas kernels, far_attention(): pl.pallas_call(functools.partial(far_kernel, head_dim=head_dim), grid_spe...  24.8 us
    ppermute x8, starting transfers between devices, partner(): lax.ppermute(x, axis, [(i, i ^ 1 << stride) for i in range(lax.axis_size(...  23 us
    pallas_call x2, Pallas kernels, near_attention(): pl.pallas_call(functools.partial(near_kernel, head_dim=head_dim), grid=(w...  10.8 us
    dot_general x2, matrix products, one_sample(): jnp.einsum('std,df->stf', inner, w_up, preferred_element_type=jnp.float32)  5.74 us
    ppermute x6, starting transfers between devices, tp_swap(): return lax.ppermute(x, 'tp', [(0, 1), (1, 0)])  5.28 us
    dot_general x2, matrix products, one_sample(): jnp.einsum('stf,fd->std', hidden, w_down_own, preferred_element_type=jnp....  4.56 us
  transfers between devices with their start and end apart: 15, of which 11 were waited for; matrix products, arithmetic and copies ran while one was open for 16% of the time, Pallas kernels for 14%

profile of v1, /device:TPU:34, one launch (start us, length us, event | category | flops | bytes accessed | tf_op | source)
XLA Modules:
  0.0 169.1 jit_solution(12551032534828848206)
XLA Ops:
  3.7 8.5 %collective-permute-done = bf16[1,384,512]{2,1,0:T(8,128)(2,1)} collective-permute-done((bf16[1,384,512]{2,1,0:T(8,128)(2,1)S(1)}, bf16[1,384,512]{2,1,0:T(8,128)(2,1)}, u32[]{:S(2)}, u32[]{:S(2)}) %collective-permute-start) | collective-permute-done | bytes 393248 | tf_op jit(solution)/shard_map/ppermute | solution.py:23
  12.2 2.1 %broadcast_select_fusion.3 = (bf16[1,384,512]{2,1,0:T(8,128)(2,1)S(1)}, bf16[1,384,512]{2,1,0:T(8,128)(2,1)S(1)}, bf16[1,384,512]{2,1,0:T(8,128)(2,1)}) fusion(bf16[1,384,512]{2,1,0:T(8,128)(2,1)} %collective-permute-done, pred[]{:T(512)S(6)} %eq.5, bf16[2,384,512]{2,1,0:T(8,128)(2,1)} %param.7), kind=kLoop, calls=%fused_computation.84 | loop fusion | flops 393216 | bytes 2359297 | tf_op jit(solution)/shard_map/jit(_where)/select_n | solution.py:39
  17.3 3.2 %collective-permute-start.1 = (bf16[2,1,384,512]{3,2,1,0:T(8,128)(2,1)}, bf16[2,1,384,512]{3,2,1,0:T(8,128)(2,1)}, u32[]{:S(2)}, u32[]{:S(2)}) collective-permute-start(bf16[2,1,384,512]{3,2,1,0:T(8,128)(2,1)} %stack.8.kn_ref.vn_ref), channel_id=1, source_target_pairs={{0,128},{2,130},{4,132},{6,134},{8,136},{10,138},{12,140},{14,142}... | collective-permute-start | bytes 2359304 | tf_op jit(solution)/shard_map/ppermute | solution.py:19
  20.5 2.1 %collective-permute-start.2 = (bf16[2,1,384,512]{3,2,1,0:T(8,128)(2,1)}, bf16[2,1,384,512]{3,2,1,0:T(8,128)(2,1)}, u32[]{:S(2)}, u32[]{:S(2)}) collective-permute-start(bf16[2,1,384,512]{3,2,1,0:T(8,128)(2,1)} %stack.8.kn_ref.vn_ref), channel_id=1, source_target_pairs={{0,64},{2,66},{4,68},{6,70},{8,72},{10,74},{12,76},{14,78},{16,80}... | collective-permute-start | bytes 2359304 | tf_op jit(solution)/shard_map/ppermute | solution.py:19
  24.1 6.3 %collective-permute-start.4 = (bf16[2,1,384,512]{3,2,1,0:T(8,128)(2,1)}, bf16[2,1,384,512]{3,2,1,0:T(8,128)(2,1)}, u32[]{:S(2)}, u32[]{:S(2)}) collective-permute-start(bf16[2,1,384,512]{3,2,1,0:T(8,128)(2,1)} %stack.8.kn_ref.vn_ref), channel_id=1, source_target_pairs={{0,16},{2,18},{4,20},{6,22},{8,24},{10,26},{12,28},{14,30},{16,0},... | collective-permute-start | bytes 2359304 | tf_op jit(solution)/shard_map/ppermute | solution.py:19
  33.4 5.4 %shard_map.73 = (f32[1,384,512]{2,1,0:T(8,128)}, f32[1,384,512]{2,1,0:T(8,128)}, f32[1,384,512]{2,1,0:T(8,128)}) custom-call(bf16[1,384,512]{2,1,0:T(8,128)(2,1)} %slice_bitcast_fusion.1.q_ref, bf16[2,1,384,512]{3,2,1,0:T(8,128)(2,1)} %stack.8.kn_ref.vn_ref, bf16[2,1,384,512]{3,2,1,0:T(8,128)(2,1)} %stack.8.kn_ref.vn_ref), custom_call_target="tpu_custom_call" | custom-call | tf_op jit(solution)/shard_map/pallas_call | solution.py:125
  38.8 7.5 %collective-permute-done.8 = bf16[1,384,512]{2,1,0:T(8,128)(2,1)} collective-permute-done((bf16[1,384,512]{2,1,0:T(8,128)(2,1)}, bf16[1,384,512]{2,1,0:T(8,128)(2,1)}, u32[]{:S(2)}, u32[]{:S(2)}) %collective-permute-start.8) | collective-permute-done | bytes 393248 | tf_op jit(solution)/shard_map/ppermute | solution.py:23
  48.7 8.6 %collective-permute-done.3 = bf16[2,1,384,512]{3,2,1,0:T(8,128)(2,1)} collective-permute-done((bf16[2,1,384,512]{3,2,1,0:T(8,128)(2,1)}, bf16[2,1,384,512]{3,2,1,0:T(8,128)(2,1)}, u32[]{:S(2)}, u32[]{:S(2)}) %collective-permute-start.3) | collective-permute-done | bytes 786464 | tf_op jit(solution)/shard_map/ppermute | solution.py:19
  57.4 6.2 %collective-permute-done.4 = bf16[2,1,384,512]{3,2,1,0:T(8,128)(2,1)} collective-permute-done((bf16[2,1,384,512]{3,2,1,0:T(8,128)(2,1)}, bf16[2,1,384,512]{3,2,1,0:T(8,128)(2,1)}, u32[]{:S(2)}, u32[]{:S(2)}) %collective-permute-start.4) | collective-permute-done | bytes 786464 | tf_op jit(solution)/shard_map/ppermute | solution.py:19
  63.6 12.4 %shard_map.74 = bf16[1,384,512]{2,1,0:T(8,128)(2,1)} custom-call(s32[12]{0:T(128)} %reshape.292.off_ref, bf16[1,384,512]{2,1,0:T(8,128)(2,1)} %slice_bitcast_fusion.1.q_ref, f32[1,384,512]{2,1,0:T(8,128)} %get-tuple-element.11.on_ref, f32[1,384,512]{2,1,0:T(8,128)} %get-tuple-element.12.mn_ref, f32[1,384,512]{2,1,0:T(8,128)} %get-tuple-element.13.ln_ref, ...), custom_call_target="tpu_custom_call" | custom-call | tf_op jit(solution)/shard_map/pallas_call | solution.py:160
  76.7 2.6 %fusion.27 = bf16[3,1,384,512]{3,2,1,0:T(8,128)(2,1)S(1)} fusion(bf16[3,1024,512]{2,1,0:T(8,128)(2,1)S(1)} %copy-done, f32[1024]{0:T(1024)S(1)} %bitcast.90, f32[384]{0:T(512)S(1)} %add_rsqrt_fusion.1, bf16[384,512]{1,0:T(8,128)(2,1)} %bitcast.88, bf16[384,512]{1,0:T(8,128)(2,1)} %bitcast.86), kind=kOutput, calls=%fused_computation.41 | convolution fusion | flops 1211301888 | bytes 5117440 | tf_op jit(solution)/shard_map/std,cde->cste/dot_general | solution.py:206
  82.3 2.3 %collective-permute-start.11 = (bf16[2,1,384,512]{3,2,1,0:T(8,128)(2,1)}, bf16[2,1,384,512]{3,2,1,0:T(8,128)(2,1)}, u32[]{:S(2)}, u32[]{:S(2)}) collective-permute-start(bf16[2,1,384,512]{3,2,1,0:T(8,128)(2,1)} %stack.9.kn_ref.vn_ref), channel_id=1, source_target_pairs={{0,32},{2,34},{4,36},{6,38},{8,40},{10,42},{12,44},{14,46},{16,48}... | collective-permute-start | bytes 2359304 | tf_op jit(solution)/shard_map/ppermute | solution.py:19
  85.5 5.4 %shard_map.75 = (f32[1,384,512]{2,1,0:T(8,128)}, f32[1,384,512]{2,1,0:T(8,128)}, f32[1,384,512]{2,1,0:T(8,128)}) custom-call(bf16[1,384,512]{2,1,0:T(8,128)(2,1)} %slice_bitcast_fusion.q_ref, bf16[2,1,384,512]{3,2,1,0:T(8,128)(2,1)} %stack.9.kn_ref.vn_ref, bf16[2,1,384,512]{3,2,1,0:T(8,128)(2,1)} %stack.9.kn_ref.vn_ref), custom_call_target="tpu_custom_call" | custom-call | tf_op jit(solution)/shard_map/pallas_call | solution.py:125
  90.9 5.5 %collective-permute-start.12 = (bf16[2,1,384,512]{3,2,1,0:T(8,128)(2,1)}, bf16[2,1,384,512]{3,2,1,0:T(8,128)(2,1)}, u32[]{:S(2)}, u32[]{:S(2)}) collective-permute-start(bf16[2,1,384,512]{3,2,1,0:T(8,128)(2,1)} %stack.9.kn_ref.vn_ref), channel_id=1, source_target_pairs={{0,16},{2,18},{4,20},{6,22},{8,24},{10,26},{12,28},{14,30},{16,0},... | collective-permute-start | bytes 2359304 | tf_op jit(solution)/shard_map/ppermute | solution.py:19
  96.5 1.9 %fusion.77 = f32[384,1024]{1,0:T(8,128)S(1)} fusion(bf16[512,1024]{1,0:T(8,128)(2,1)} %collective-permute-done.6, bf16[1,384,512]{2,1,0:T(8,128)(2,1)} %collective-permute-done.5), kind=kOutput, calls=%fused_computation.78 | convolution fusion | flops 402653184 | bytes 3014656 | tf_op jit(solution)/shard_map/sth,hd->std/dot_general | solution.py:226
  100.0 2.5 %collective-permute-done.9 = bf16[2,1,384,512]{3,2,1,0:T(8,128)(2,1)} collective-permute-done((bf16[2,1,384,512]{3,2,1,0:T(8,128)(2,1)}, bf16[2,1,384,512]{3,2,1,0:T(8,128)(2,1)}, u32[]{:S(2)}, u32[]{:S(2)}) %collective-permute-start.9) | collective-permute-done | bytes 786464 | tf_op jit(solution)/shard_map/ppermute | solution.py:19
  104.3 12.2 %collective-permute-done.11 = bf16[2,1,384,512]{3,2,1,0:T(8,128)(2,1)} collective-permute-done((bf16[2,1,384,512]{3,2,1,0:T(8,128)(2,1)}, bf16[2,1,384,512]{3,2,1,0:T(8,128)(2,1)}, u32[]{:S(2)}, u32[]{:S(2)}) %collective-permute-start.11) | collective-permute-done | bytes 786464 | tf_op jit(solution)/shard_map/ppermute | solution.py:19
  116.5 8.3 %collective-permute-done.12 = bf16[2,1,384,512]{3,2,1,0:T(8,128)(2,1)} collective-permute-done((bf16[2,1,384,512]{3,2,1,0:T(8,128)(2,1)}, bf16[2,1,384,512]{3,2,1,0:T(8,128)(2,1)}, u32[]{:S(2)}, u32[]{:S(2)}) %collective-permute-start.12) | collective-permute-done | bytes 786464 | tf_op jit(solution)/shard_map/ppermute | solution.py:19
  124.8 12.4 %shard_map.76 = bf16[1,384,512]{2,1,0:T(8,128)(2,1)} custom-call(s32[12]{0:T(128)} %reshape.292.off_ref, bf16[1,384,512]{2,1,0:T(8,128)(2,1)} %slice_bitcast_fusion.q_ref, f32[1,384,512]{2,1,0:T(8,128)} %get-tuple-element.14.on_ref, f32[1,384,512]{2,1,0:T(8,128)} %get-tuple-element.15.mn_ref, f32[1,384,512]{2,1,0:T(8,128)} %get-tuple-element.16.ln_ref, ...), custom_call_target="tpu_custom_call" | custom-call | tf_op jit(solution)/shard_map/pallas_call | solution.py:160
  137.3 4.0 %fusion.7 = bf16[384,1536]{1,0:T(8,128)(2,1)S(1)} fusion(bf16[1024,1536]{1,0:T(8,128)(2,1)} %param.12, bf16[384,1024]{1,0:T(8,128)(2,1)} %get-tuple-element.29, f32[384]{0:T(512)S(1)} %add_rsqrt_fusion.2), kind=kOutput, calls=%fused_computation.9 | convolution fusion | flops 1214447616 | bytes 5113344 | tf_op jit(solution)/shard_map/std,df->stf/dot_general | solution.py:233
  142.9 2.1 %collective-permute-start.7 = (bf16[1,384,512]{2,1,0:T(8,128)(2,1)}, bf16[1,384,512]{2,1,0:T(8,128)(2,1)S(1)}, u32[]{:S(2)}, u32[]{:S(2)}) collective-permute-start(bf16[1,384,512]{2,1,0:T(8,128)(2,1)} %fusion.51), channel_id=1, source_target_pairs={{0,1},{1,0},{2,3},{3,2},{4,5},{5,4},{6,7},{7,6},{8,9},{9,8},{10,11... | collective-permute-start | bytes 1179656 | tf_op jit(solution)/shard_map/ppermute | solution.py:23
  145.0 4.4 %collective-permute-done.13 = bf16[1,384,512]{2,1,0:T(8,128)(2,1)S(1)} collective-permute-done((bf16[1,384,512]{2,1,0:T(8,128)(2,1)}, bf16[1,384,512]{2,1,0:T(8,128)(2,1)S(1)}, u32[]{:S(2)}, u32[]{:S(2)}) %collective-permute-start.13) | collective-permute-done | bytes 393248 | tf_op jit(solution)/shard_map/ppermute | solution.py:23
  156.9 2.8 %fusion.67 = bf16[1,384,512]{2,1,0:T(8,128)(2,1)S(1)} fusion(bf16[1,384,512]{2,1,0:T(8,128)(2,1)S(1)} %collective-permute-done.7, bf16[384,1024]{1,0:T(8,128)(2,1)} %get-tuple-element.29, s32[]{:T(128)S(6)} %select_n.41, bf16[384,1536]{1,0:T(8,128)(2,1)} %copy-done.18, bf16[1536,1024]{1,0:T(8,128)(2,1)} %param.13), kind=kOutput, calls=%fused_computation.66 | convolution fusion | flops 604962816 | bytes 3933184 | tf_op jit(solution)/shard_map/stf,fd->std/dot_general | solution.py:240
  159.7 6.6 %collective-permute-done.14 = bf16[1,384,512]{2,1,0:T(8,128)(2,1)} collective-permute-done((bf16[1,384,512]{2,1,0:T(8,128)(2,1)}, bf16[1,384,512]{2,1,0:T(8,128)(2,1)}, u32[]{:S(2)}, u32[]{:S(2)}) %collective-permute-start.14) | collective-permute-done | bytes 393248 | tf_op jit(solution)/shard_map/ppermute | solution.py:23
  (84 shorter events, 33.3 us)
Async XLA Ops:
  0.0 14.6 %copy-start = (bf16[3,1024,512]{2,1,0:T(8,128)(2,1)S(1)}, bf16[3,1024,512]{2,1,0:T(8,128)(2,1)}, u32[]{:S(2)}) copy-start(bf16[3,1024,512]{2,1,0:T(8,128)(2,1)} %param.10) | copy-start | bytes 9437188
  1.2 11.0 %collective-permute-start = (bf16[1,384,512]{2,1,0:T(8,128)(2,1)S(1)}, bf16[1,384,512]{2,1,0:T(8,128)(2,1)}, u32[]{:S(2)}, u32[]{:S(2)}) collective-permute-start(bf16[1,384,512]{2,1,0:T(8,128)(2,1)S(1)} %slice.28), channel_id=1, source_target_pairs={{0,1},{1,0},{2,3},{3,2},{4,5},{5,4},{6,7},{7,6},{8,9},{9,8},{10,11... | collective-permute-start | bytes 1179656 | tf_op jit(solution)/shard_map/ppermute | solution.py:23
  16.0 15.0 %copy-start.10 = (s32[3,4]{1,0:T(4,128)S(1)}, s32[3,4]{1,0:T(4,128)}, u32[]{:S(2)}) copy-start(s32[3,4]{1,0:T(4,128)} %param.9) | copy-start | bytes 148
  17.3 31.4 %collective-permute-start.1 = (bf16[2,1,384,512]{3,2,1,0:T(8,128)(2,1)}, bf16[2,1,384,512]{3,2,1,0:T(8,128)(2,1)}, u32[]{:S(2)}, u32[]{:S(2)}) collective-permute-start(bf16[2,1,384,512]{3,2,1,0:T(8,128)(2,1)} %stack.8.kn_ref.vn_ref), channel_id=1, source_target_pairs={{0,128},{2,130},{4,132},{6,134},{8,136},{10,138},{12,140},{14,142}... | collective-permute-start | bytes 2359304 | tf_op jit(solution)/shard_map/ppermute | solution.py:19
  20.5 28.2 %collective-permute-start.2 = (bf16[2,1,384,512]{3,2,1,0:T(8,128)(2,1)}, bf16[2,1,384,512]{3,2,1,0:T(8,128)(2,1)}, u32[]{:S(2)}, u32[]{:S(2)}) collective-permute-start(bf16[2,1,384,512]{3,2,1,0:T(8,128)(2,1)} %stack.8.kn_ref.vn_ref), channel_id=1, source_target_pairs={{0,64},{2,66},{4,68},{6,70},{8,72},{10,74},{12,76},{14,78},{16,80}... | collective-permute-start | bytes 2359304 | tf_op jit(solution)/shard_map/ppermute | solution.py:19
  22.6 34.7 %collective-permute-start.3 = (bf16[2,1,384,512]{3,2,1,0:T(8,128)(2,1)}, bf16[2,1,384,512]{3,2,1,0:T(8,128)(2,1)}, u32[]{:S(2)}, u32[]{:S(2)}) collective-permute-start(bf16[2,1,384,512]{3,2,1,0:T(8,128)(2,1)} %stack.8.kn_ref.vn_ref), channel_id=1, source_target_pairs={{0,32},{2,34},{4,36},{6,38},{8,40},{10,42},{12,44},{14,46},{16,48}... | collective-permute-start | bytes 2359304 | tf_op jit(solution)/shard_map/ppermute | solution.py:19
  24.1 39.5 %collective-permute-start.4 = (bf16[2,1,384,512]{3,2,1,0:T(8,128)(2,1)}, bf16[2,1,384,512]{3,2,1,0:T(8,128)(2,1)}, u32[]{:S(2)}, u32[]{:S(2)}) collective-permute-start(bf16[2,1,384,512]{3,2,1,0:T(8,128)(2,1)} %stack.8.kn_ref.vn_ref), channel_id=1, source_target_pairs={{0,16},{2,18},{4,20},{6,22},{8,24},{10,26},{12,28},{14,30},{16,0},... | collective-permute-start | bytes 2359304 | tf_op jit(solution)/shard_map/ppermute | solution.py:19
  30.4 16.0 %collective-permute-start.8 = (bf16[1,384,512]{2,1,0:T(8,128)(2,1)}, bf16[1,384,512]{2,1,0:T(8,128)(2,1)}, u32[]{:S(2)}, u32[]{:S(2)}) collective-permute-start(bf16[1,384,512]{2,1,0:T(8,128)(2,1)} %get-tuple-element.21), channel_id=1, source_target_pairs={{0,1},{1,0},{2,3},{3,2},{4,5},{5,4},{6,7},{7,6},{8,9},{9,8},{10,11... | collective-permute-start | bytes 1179656 | tf_op jit(solution)/shard_map/ppermute | solution.py:23
  46.3 44.6 %collective-permute-start.6 = (bf16[512,1024]{1,0:T(8,128)(2,1)}, bf16[512,1024]{1,0:T(8,128)(2,1)}, u32[]{:S(2)}, u32[]{:S(2)}) collective-permute-start(bf16[512,1024]{1,0:T(8,128)(2,1)} %param.11), channel_id=1, source_target_pairs={{0,129},{1,128},{2,131},{3,130},{4,133},{5,132},{6,135},{7,134},{8... | collective-permute-start | bytes 3145736 | tf_op jit(solution)/shard_map/ppermute | solution.py:35
  76.0 20.5 %collective-permute-start.5 = (bf16[1,384,512]{2,1,0:T(8,128)(2,1)}, bf16[1,384,512]{2,1,0:T(8,128)(2,1)}, u32[]{:S(2)}, u32[]{:S(2)}) collective-permute-start(bf16[1,384,512]{2,1,0:T(8,128)(2,1)} %shard_map.74), channel_id=1, source_target_pairs={{0,1},{1,0},{2,3},{3,2},{4,5},{5,4},{6,7},{7,6},{8,9},{9,8},{10,11... | collective-permute-start | bytes 1179656 | tf_op jit(solution)/shard_map/ppermute | solution.py:23
  80.2 22.3 %collective-permute-start.9 = (bf16[2,1,384,512]{3,2,1,0:T(8,128)(2,1)}, bf16[2,1,384,512]{3,2,1,0:T(8,128)(2,1)}, u32[]{:S(2)}, u32[]{:S(2)}) collective-permute-start(bf16[2,1,384,512]{3,2,1,0:T(8,128)(2,1)} %stack.9.kn_ref.vn_ref), channel_id=1, source_target_pairs={{0,128},{2,130},{4,132},{6,134},{8,136},{10,138},{12,140},{14,142}... | collective-permute-start | bytes 2359304 | tf_op jit(solution)/shard_map/ppermute | solution.py:19
  82.1 22.2 %collective-permute-start.10 = (bf16[2,1,384,512]{3,2,1,0:T(8,128)(2,1)}, bf16[2,1,384,512]{3,2,1,0:T(8,128)(2,1)}, u32[]{:S(2)}, u32[]{:S(2)}) collective-permute-start(bf16[2,1,384,512]{3,2,1,0:T(8,128)(2,1)} %stack.9.kn_ref.vn_ref), channel_id=1, source_target_pairs={{0,64},{2,66},{4,68},{6,70},{8,72},{10,74},{12,76},{14,78},{16,80}... | collective-permute-start | bytes 2359304 | tf_op jit(solution)/shard_map/ppermute | solution.py:19
  82.3 34.2 %collective-permute-start.11 = (bf16[2,1,384,512]{3,2,1,0:T(8,128)(2,1)}, bf16[2,1,384,512]{3,2,1,0:T(8,128)(2,1)}, u32[]{:S(2)}, u32[]{:S(2)}) collective-permute-start(bf16[2,1,384,512]{3,2,1,0:T(8,128)(2,1)} %stack.9.kn_ref.vn_ref), channel_id=1, source_target_pairs={{0,32},{2,34},{4,36},{6,38},{8,40},{10,42},{12,44},{14,46},{16,48}... | collective-permute-start | bytes 2359304 | tf_op jit(solution)/shard_map/ppermute | solution.py:19
  90.9 33.8 %collective-permute-start.12 = (bf16[2,1,384,512]{3,2,1,0:T(8,128)(2,1)}, bf16[2,1,384,512]{3,2,1,0:T(8,128)(2,1)}, u32[]{:S(2)}, u32[]{:S(2)}) collective-permute-start(bf16[2,1,384,512]{3,2,1,0:T(8,128)(2,1)} %stack.9.kn_ref.vn_ref), channel_id=1, source_target_pairs={{0,16},{2,18},{4,20},{6,22},{8,24},{10,26},{12,28},{14,30},{16,0},... | collective-permute-start | bytes 2359304 | tf_op jit(solution)/shard_map/ppermute | solution.py:19
  137.1 12.3 %collective-permute-start.13 = (bf16[1,384,512]{2,1,0:T(8,128)(2,1)}, bf16[1,384,512]{2,1,0:T(8,128)(2,1)S(1)}, u32[]{:S(2)}, u32[]{:S(2)}) collective-permute-start(bf16[1,384,512]{2,1,0:T(8,128)(2,1)} %shard_map.76), channel_id=1, source_target_pairs={{0,1},{1,0},{2,3},{3,2},{4,5},{5,4},{6,7},{7,6},{8,9},{9,8},{10,11... | collective-permute-start | bytes 1179656 | tf_op jit(solution)/shard_map/ppermute | solution.py:23
  142.9 8.4 %copy-start.4 = (bf16[1,384,512]{2,1,0:T(8,128)(2,1)S(1)}, bf16[1,384,512]{2,1,0:T(8,128)(2,1)}, u32[]{:S(2)}) copy-start(bf16[1,384,512]{2,1,0:T(8,128)(2,1)} %copy-done.3) | copy-start | bytes 1179652
  142.9 8.4 %copy-start.6 = (bf16[1,384,512]{2,1,0:T(8,128)(2,1)S(1)}, bf16[1,384,512]{2,1,0:T(8,128)(2,1)}, u32[]{:S(2)}) copy-start(bf16[1,384,512]{2,1,0:T(8,128)(2,1)} %copy-done.5) | copy-start | bytes 1179652
  142.9 8.4 %copy-start.9 = (bf16[1,384,512]{2,1,0:T(8,128)(2,1)S(1)}, bf16[1,384,512]{2,1,0:T(8,128)(2,1)}, u32[]{:S(2)}) copy-start(bf16[1,384,512]{2,1,0:T(8,128)(2,1)} %shard_map.76) | copy-start | bytes 1179652
  142.9 8.4 %copy-start.15 = (bf16[512,1024]{1,0:T(8,128)(2,1)S(1)}, bf16[512,1024]{1,0:T(8,128)(2,1)}, u32[]{:S(2)}) copy-start(bf16[512,1024]{1,0:T(8,128)(2,1)} %param.11) | copy-start | bytes 3145732
  142.9 14.0 %collective-permute-start.7 = (bf16[1,384,512]{2,1,0:T(8,128)(2,1)}, bf16[1,384,512]{2,1,0:T(8,128)(2,1)S(1)}, u32[]{:S(2)}, u32[]{:S(2)}) collective-permute-start(bf16[1,384,512]{2,1,0:T(8,128)(2,1)} %fusion.51), channel_id=1, source_target_pairs={{0,1},{1,0},{2,3},{3,2},{4,5},{5,4},{6,7},{7,6},{8,9},{9,8},{10,11... | collective-permute-start | bytes 1179656 | tf_op jit(solution)/shard_map/ppermute | solution.py:23
  156.8 9.5 %collective-permute-start.14 = (bf16[1,384,512]{2,1,0:T(8,128)(2,1)}, bf16[1,384,512]{2,1,0:T(8,128)(2,1)}, u32[]{:S(2)}, u32[]{:S(2)}) collective-permute-start(bf16[1,384,512]{2,1,0:T(8,128)(2,1)} %fusion.48), channel_id=1, source_target_pairs={{0,1},{1,0},{2,3},{3,2},{4,5},{5,4},{6,7},{7,6},{8,9},{9,8},{10,11... | collective-permute-start | bytes 1179656 | tf_op jit(solution)/shard_map/ppermute | solution.py:23
  156.8 9.5 %copy-start.13 = (bf16[1536,1024]{1,0:T(8,128)(2,1)S(1)}, bf16[1536,1024]{1,0:T(8,128)(2,1)}, u32[]{:S(2)}) copy-start(bf16[1536,1024]{1,0:T(8,128)(2,1)} %param.13) | copy-start | bytes 9437188
  156.8 9.5 %copy-start.17 = (bf16[384,1024]{1,0:T(8,128)(2,1)S(1)}, bf16[384,1024]{1,0:T(8,128)(2,1)}, u32[]{:S(2)}) copy-start(bf16[384,1024]{1,0:T(8,128)(2,1)} %copy-done.16) | copy-start | bytes 2359300
  156.8 9.5 %copy-start.20 = (bf16[384,1536]{1,0:T(8,128)(2,1)S(1)}, bf16[384,1536]{1,0:T(8,128)(2,1)}, u32[]{:S(2)}) copy-start(bf16[384,1536]{1,0:T(8,128)(2,1)} %copy-done.19) | copy-start | bytes 3538948
  (12 other events, 39.7 us)

commit v2 on v1

--- a/solution.py
+++ b/solution.py
@@ -61,7 +61,7 @@
         total = expd.sum(axis=-1, keepdims=True)
         mixed = jnp.dot(expd.astype(jnp.bfloat16), value_near, preferred_element_type=jnp.float32)
         parts.append((mixed, top, total))
-    o_ref[0] = jnp.where(first, parts[0][0], parts[1][0])
+    o_ref[0] = jnp.where(first, parts[0][0], parts[1][0]).astype(o_ref.dtype)
     m_ref[0] = jnp.where(first, parts[0][1], parts[1][1])
     l_ref[0] = jnp.where(first, parts[0][2], parts[1][2])
 
@@ -107,7 +107,7 @@
     far_o = jnp.where(first, parts[0][0], parts[1][0])
     far_m = jnp.where(first, parts[0][1], parts[1][1])
     far_l = jnp.where(first, parts[0][2], parts[1][2])
-    near_o = on_ref[0]
+    near_o = on_ref[0].astype(jnp.float32)
     near_m = mn_ref[0]
     near_l = ln_ref[0]
     top = jnp.maximum(near_m, far_m)
@@ -122,6 +122,7 @@
     lanes = 2 * head_dim
     row_spec = pl.BlockSpec((1, tok_rows, lanes), lambda j: (0, 0, j))
     stat = jax.ShapeDtypeStruct(queries.shape, jnp.float32)
+    part = jax.ShapeDtypeStruct(queries.shape, jnp.bfloat16)
     return pl.pallas_call(
         functools.partial(near_kernel, head_dim=head_dim),
         grid=(width // lanes,),
@@ -131,7 +132,7 @@
             pl.BlockSpec((1, 1, tok_rows, lanes), lambda j: (1, 0, 0, j)),
         ],
         out_specs=[row_spec, row_spec, row_spec],
-        out_shape=[stat, stat, stat],
+        out_shape=[part, stat, stat],
     )(queries, kv_here, kv_here)
 
 

time: 170 us -> 170 us (level)
  no operation moved by 1% of the time
where the time goes in v2:
time: 170 us; the launch traced here: 169 us
  waiting for transfers between devices  66.8 us (39%)
  Pallas kernels  35.5 us (21%)
  starting transfers between devices  28.5 us (17%)
  matrix products  23.6 us (14%)
  local copies, waits for them, and re-layouts  8.74 us (5%)
  other arithmetic  5.52 us (3%)
    ppermute x8, waiting for transfers between devices, partner(): lax.ppermute(x, axis, [(i, i ^ 1 << stride) for i in range(lax.axis_size(...  39.6 us
    ppermute x6, waiting for transfers between devices, tp_swap(): return lax.ppermute(x, 'tp', [(0, 1), (1, 0)])  27.3 us
    pallas_call x2, Pallas kernels, far_attention(): pl.pallas_call(functools.partial(far_kernel, head_dim=head_dim), grid_spe...  24.8 us
    ppermute x8, starting transfers between devices, partner(): lax.ppermute(x, axis, [(i, i ^ 1 << stride) for i in range(lax.axis_size(...  23 us
    pallas_call x2, Pallas kernels, near_attention(): pl.pallas_call(functools.partial(near_kernel, head_dim=head_dim), grid=(w...  10.7 us
    dot_general x2, matrix products, one_sample(): jnp.einsum('std,df->stf', inner, w_up, preferred_element_type=jnp.float32)  5.74 us
    ppermute x6, starting transfers between devices, tp_swap(): return lax.ppermute(x, 'tp', [(0, 1), (1, 0)])  5.28 us
    dot_general x2, matrix products, one_sample(): jnp.einsum('stf,fd->std', hidden, w_down_own, preferred_element_type=jnp....  4.56 us
  transfers between devices with their start and end apart: 15, of which 11 were waited for; matrix products, arithmetic and copies ran while one was open for 16% of the time, Pallas kernels for 14%

profile of v2, /device:TPU:34, one launch (start us, length us, event | category | flops | bytes accessed | tf_op | source)
XLA Modules:
  0.0 169.0 jit_solution(2551852780921214634)
XLA Ops:
  3.7 8.5 %collective-permute-done = bf16[1,384,512]{2,1,0:T(8,128)(2,1)} collective-permute-done((bf16[1,384,512]{2,1,0:T(8,128)(2,1)S(1)}, bf16[1,384,512]{2,1,0:T(8,128)(2,1)}, u32[]{:S(2)}, u32[]{:S(2)}) %collective-permute-start) | collective-permute-done | bytes 393248 | tf_op jit(solution)/shard_map/ppermute | solution.py:23
  12.2 2.1 %broadcast_select_fusion.3 = (bf16[1,384,512]{2,1,0:T(8,128)(2,1)S(1)}, bf16[1,384,512]{2,1,0:T(8,128)(2,1)S(1)}, bf16[1,384,512]{2,1,0:T(8,128)(2,1)}) fusion(bf16[1,384,512]{2,1,0:T(8,128)(2,1)} %collective-permute-done, pred[]{:T(512)S(6)} %eq.5, bf16[2,384,512]{2,1,0:T(8,128)(2,1)} %param.7), kind=kLoop, calls=%fused_computation.84 | loop fusion | flops 393216 | bytes 2359297 | tf_op jit(solution)/shard_map/jit(_where)/select_n | solution.py:39
  17.3 3.2 %collective-permute-start.1 = (bf16[2,1,384,512]{3,2,1,0:T(8,128)(2,1)}, bf16[2,1,384,512]{3,2,1,0:T(8,128)(2,1)}, u32[]{:S(2)}, u32[]{:S(2)}) collective-permute-start(bf16[2,1,384,512]{3,2,1,0:T(8,128)(2,1)} %stack.8.kn_ref.vn_ref), channel_id=1, source_target_pairs={{0,128},{2,130},{4,132},{6,134},{8,136},{10,138},{12,140},{14,142}... | collective-permute-start | bytes 2359304 | tf_op jit(solution)/shard_map/ppermute | solution.py:19
  20.5 2.1 %collective-permute-start.2 = (bf16[2,1,384,512]{3,2,1,0:T(8,128)(2,1)}, bf16[2,1,384,512]{3,2,1,0:T(8,128)(2,1)}, u32[]{:S(2)}, u32[]{:S(2)}) collective-permute-start(bf16[2,1,384,512]{3,2,1,0:T(8,128)(2,1)} %stack.8.kn_ref.vn_ref), channel_id=1, source_target_pairs={{0,64},{2,66},{4,68},{6,70},{8,72},{10,74},{12,76},{14,78},{16,80}... | collective-permute-start | bytes 2359304 | tf_op jit(solution)/shard_map/ppermute | solution.py:19
  24.1 6.3 %collective-permute-start.4 = (bf16[2,1,384,512]{3,2,1,0:T(8,128)(2,1)}, bf16[2,1,384,512]{3,2,1,0:T(8,128)(2,1)}, u32[]{:S(2)}, u32[]{:S(2)}) collective-permute-start(bf16[2,1,384,512]{3,2,1,0:T(8,128)(2,1)} %stack.8.kn_ref.vn_ref), channel_id=1, source_target_pairs={{0,16},{2,18},{4,20},{6,22},{8,24},{10,26},{12,28},{14,30},{16,0},... | collective-permute-start | bytes 2359304 | tf_op jit(solution)/shard_map/ppermute | solution.py:19
  33.4 5.4 %shard_map.73 = (bf16[1,384,512]{2,1,0:T(8,128)(2,1)}, f32[1,384,512]{2,1,0:T(8,128)}, f32[1,384,512]{2,1,0:T(8,128)}) custom-call(bf16[1,384,512]{2,1,0:T(8,128)(2,1)} %slice_bitcast_fusion.1.q_ref, bf16[2,1,384,512]{3,2,1,0:T(8,128)(2,1)} %stack.8.kn_ref.vn_ref, bf16[2,1,384,512]{3,2,1,0:T(8,128)(2,1)} %stack.8.kn_ref.vn_ref), custom_call_target="tpu_custom_call" | custom-call | tf_op jit(solution)/shard_map/pallas_call | solution.py:126
  38.8 7.5 %collective-permute-done.8 = bf16[1,384,512]{2,1,0:T(8,128)(2,1)} collective-permute-done((bf16[1,384,512]{2,1,0:T(8,128)(2,1)}, bf16[1,384,512]{2,1,0:T(8,128)(2,1)}, u32[]{:S(2)}, u32[]{:S(2)}) %collective-permute-start.8) | collective-permute-done | bytes 393248 | tf_op jit(solution)/shard_map/ppermute | solution.py:23
  48.7 8.6 %collective-permute-done.3 = bf16[2,1,384,512]{3,2,1,0:T(8,128)(2,1)} collective-permute-done((bf16[2,1,384,512]{3,2,1,0:T(8,128)(2,1)}, bf16[2,1,384,512]{3,2,1,0:T(8,128)(2,1)}, u32[]{:S(2)}, u32[]{:S(2)}) %collective-permute-start.3) | collective-permute-done | bytes 786464 | tf_op jit(solution)/shard_map/ppermute | solution.py:19
  57.4 6.2 %collective-permute-done.4 = bf16[2,1,384,512]{3,2,1,0:T(8,128)(2,1)} collective-permute-done((bf16[2,1,384,512]{3,2,1,0:T(8,128)(2,1)}, bf16[2,1,384,512]{3,2,1,0:T(8,128)(2,1)}, u32[]{:S(2)}, u32[]{:S(2)}) %collective-permute-start.4) | collective-permute-done | bytes 786464 | tf_op jit(solution)/shard_map/ppermute | solution.py:19
  63.6 12.4 %shard_map.74 = bf16[1,384,512]{2,1,0:T(8,128)(2,1)} custom-call(s32[12]{0:T(128)} %reshape.292.off_ref, bf16[1,384,512]{2,1,0:T(8,128)(2,1)} %slice_bitcast_fusion.1.q_ref, bf16[1,384,512]{2,1,0:T(8,128)(2,1)} %get-tuple-element.11.on_ref, f32[1,384,512]{2,1,0:T(8,128)} %get-tuple-element.12.mn_ref, f32[1,384,512]{2,1,0:T(8,128)} %get-tuple-element.13.ln_ref, ...), custom_call_target="tpu_custom_call" | custom-call | tf_op jit(solution)/shard_map/pallas_call | solution.py:161
  76.7 2.6 %fusion.27 = bf16[3,1,384,512]{3,2,1,0:T(8,128)(2,1)S(1)} fusion(bf16[3,1024,512]{2,1,0:T(8,128)(2,1)S(1)} %copy-done, f32[1024]{0:T(1024)S(1)} %bitcast.90, f32[384]{0:T(512)S(1)} %add_rsqrt_fusion.1, bf16[384,512]{1,0:T(8,128)(2,1)} %bitcast.88, bf16[384,512]{1,0:T(8,128)(2,1)} %bitcast.86), kind=kOutput, calls=%fused_computation.41 | convolution fusion | flops 1211301888 | bytes 5117440 | tf_op jit(solution)/shard_map/std,cde->cste/dot_general | solution.py:207
  82.3 2.3 %collective-permute-start.11 = (bf16[2,1,384,512]{3,2,1,0:T(8,128)(2,1)}, bf16[2,1,384,512]{3,2,1,0:T(8,128)(2,1)}, u32[]{:S(2)}, u32[]{:S(2)}) collective-permute-start(bf16[2,1,384,512]{3,2,1,0:T(8,128)(2,1)} %stack.9.kn_ref.vn_ref), channel_id=1, source_target_pairs={{0,32},{2,34},{4,36},{6,38},{8,40},{10,42},{12,44},{14,46},{16,48}... | collective-permute-start | bytes 2359304 | tf_op jit(solution)/shard_map/ppermute | solution.py:19
  85.5 5.4 %shard_map.75 = (bf16[1,384,512]{2,1,0:T(8,128)(2,1)}, f32[1,384,512]{2,1,0:T(8,128)}, f32[1,384,512]{2,1,0:T(8,128)}) custom-call(bf16[1,384,512]{2,1,0:T(8,128)(2,1)} %slice_bitcast_fusion.q_ref, bf16[2,1,384,512]{3,2,1,0:T(8,128)(2,1)} %stack.9.kn_ref.vn_ref, bf16[2,1,384,512]{3,2,1,0:T(8,128)(2,1)} %stack.9.kn_ref.vn_ref), custom_call_target="tpu_custom_call" | custom-call | tf_op jit(solution)/shard_map/pallas_call | solution.py:126
  90.9 5.5 %collective-permute-start.12 = (bf16[2,1,384,512]{3,2,1,0:T(8,128)(2,1)}, bf16[2,1,384,512]{3,2,1,0:T(8,128)(2,1)}, u32[]{:S(2)}, u32[]{:S(2)}) collective-permute-start(bf16[2,1,384,512]{3,2,1,0:T(8,128)(2,1)} %stack.9.kn_ref.vn_ref), channel_id=1, source_target_pairs={{0,16},{2,18},{4,20},{6,22},{8,24},{10,26},{12,28},{14,30},{16,0},... | collective-permute-start | bytes 2359304 | tf_op jit(solution)/shard_map/ppermute | solution.py:19
  96.4 1.9 %fusion.77 = f32[384,1024]{1,0:T(8,128)S(1)} fusion(bf16[512,1024]{1,0:T(8,128)(2,1)} %collective-permute-done.6, bf16[1,384,512]{2,1,0:T(8,128)(2,1)} %collective-permute-done.5), kind=kOutput, calls=%fused_computation.78 | convolution fusion | flops 402653184 | bytes 3014656 | tf_op jit(solution)/shard_map/sth,hd->std/dot_general | solution.py:227
  100.0 2.6 %collective-permute-done.9 = bf16[2,1,384,512]{3,2,1,0:T(8,128)(2,1)} collective-permute-done((bf16[2,1,384,512]{3,2,1,0:T(8,128)(2,1)}, bf16[2,1,384,512]{3,2,1,0:T(8,128)(2,1)}, u32[]{:S(2)}, u32[]{:S(2)}) %collective-permute-start.9) | collective-permute-done | bytes 786464 | tf_op jit(solution)/shard_map/ppermute | solution.py:19
  104.3 12.2 %collective-permute-done.11 = bf16[2,1,384,512]{3,2,1,0:T(8,128)(2,1)} collective-permute-done((bf16[2,1,384,512]{3,2,1,0:T(8,128)(2,1)}, bf16[2,1,384,512]{3,2,1,0:T(8,128)(2,1)}, u32[]{:S(2)}, u32[]{:S(2)}) %collective-permute-start.11) | collective-permute-done | bytes 786464 | tf_op jit(solution)/shard_map/ppermute | solution.py:19
  116.5 8.2 %collective-permute-done.12 = bf16[2,1,384,512]{3,2,1,0:T(8,128)(2,1)} collective-permute-done((bf16[2,1,384,512]{3,2,1,0:T(8,128)(2,1)}, bf16[2,1,384,512]{3,2,1,0:T(8,128)(2,1)}, u32[]{:S(2)}, u32[]{:S(2)}) %collective-permute-start.12) | collective-permute-done | bytes 786464 | tf_op jit(solution)/shard_map/ppermute | solution.py:19
  124.7 12.4 %shard_map.76 = bf16[1,384,512]{2,1,0:T(8,128)(2,1)} custom-call(s32[12]{0:T(128)} %reshape.292.off_ref, bf16[1,384,512]{2,1,0:T(8,128)(2,1)} %slice_bitcast_fusion.q_ref, bf16[1,384,512]{2,1,0:T(8,128)(2,1)} %get-tuple-element.14.on_ref, f32[1,384,512]{2,1,0:T(8,128)} %get-tuple-element.15.mn_ref, f32[1,384,512]{2,1,0:T(8,128)} %get-tuple-element.16.ln_ref, ...), custom_call_target="tpu_custom_call" | custom-call | tf_op jit(solution)/shard_map/pallas_call | solution.py:161
  137.2 4.0 %fusion.7 = bf16[384,1536]{1,0:T(8,128)(2,1)S(1)} fusion(bf16[1024,1536]{1,0:T(8,128)(2,1)} %param.12, bf16[384,1024]{1,0:T(8,128)(2,1)} %get-tuple-element.29, f32[384]{0:T(512)S(1)} %add_rsqrt_fusion.2), kind=kOutput, calls=%fused_computation.9 | convolution fusion | flops 1214447616 | bytes 5113344 | tf_op jit(solution)/shard_map/std,df->stf/dot_general | solution.py:234
  142.8 2.1 %collective-permute-start.7 = (bf16[1,384,512]{2,1,0:T(8,128)(2,1)}, bf16[1,384,512]{2,1,0:T(8,128)(2,1)S(1)}, u32[]{:S(2)}, u32[]{:S(2)}) collective-permute-start(bf16[1,384,512]{2,1,0:T(8,128)(2,1)} %fusion.51), channel_id=1, source_target_pairs={{0,1},{1,0},{2,3},{3,2},{4,5},{5,4},{6,7},{7,6},{8,9},{9,8},{10,11... | collective-permute-start | bytes 1179656 | tf_op jit(solution)/shard_map/ppermute | solution.py:23
  144.9 4.4 %collective-permute-done.13 = bf16[1,384,512]{2,1,0:T(8,128)(2,1)S(1)} collective-permute-done((bf16[1,384,512]{2,1,0:T(8,128)(2,1)}, bf16[1,384,512]{2,1,0:T(8,128)(2,1)S(1)}, u32[]{:S(2)}, u32[]{:S(2)}) %collective-permute-start.13) | collective-permute-done | bytes 393248 | tf_op jit(solution)/shard_map/ppermute | solution.py:23
  156.9 2.8 %fusion.67 = bf16[1,384,512]{2,1,0:T(8,128)(2,1)S(1)} fusion(bf16[1,384,512]{2,1,0:T(8,128)(2,1)S(1)} %collective-permute-done.7, bf16[384,1024]{1,0:T(8,128)(2,1)} %get-tuple-element.29, s32[]{:T(128)S(6)} %select_n.41, bf16[384,1536]{1,0:T(8,128)(2,1)} %copy-done.18, bf16[1536,1024]{1,0:T(8,128)(2,1)} %param.13), kind=kOutput, calls=%fused_computation.66 | convolution fusion | flops 604962816 | bytes 3933184 | tf_op jit(solution)/shard_map/stf,fd->std/dot_general | solution.py:241
  159.6 6.6 %collective-permute-done.14 = bf16[1,384,512]{2,1,0:T(8,128)(2,1)} collective-permute-done((bf16[1,384,512]{2,1,0:T(8,128)(2,1)}, bf16[1,384,512]{2,1,0:T(8,128)(2,1)}, u32[]{:S(2)}, u32[]{:S(2)}) %collective-permute-start.14) | collective-permute-done | bytes 393248 | tf_op jit(solution)/shard_map/ppermute | solution.py:23
  (84 shorter events, 33.3 us)
Async XLA Ops:
  0.0 14.6 %copy-start = (bf16[3,1024,512]{2,1,0:T(8,128)(2,1)S(1)}, bf16[3,1024,512]{2,1,0:T(8,128)(2,1)}, u32[]{:S(2)}) copy-start(bf16[3,1024,512]{2,1,0:T(8,128)(2,1)} %param.10) | copy-start | bytes 9437188
  1.2 11.0 %collective-permute-start = (bf16[1,384,512]{2,1,0:T(8,128)(2,1)S(1)}, bf16[1,384,512]{2,1,0:T(8,128)(2,1)}, u32[]{:S(2)}, u32[]{:S(2)}) collective-permute-start(bf16[1,384,512]{2,1,0:T(8,128)(2,1)S(1)} %slice.28), channel_id=1, source_target_pairs={{0,1},{1,0},{2,3},{3,2},{4,5},{5,4},{6,7},{7,6},{8,9},{9,8},{10,11... | collective-permute-start | bytes 1179656 | tf_op jit(solution)/shard_map/ppermute | solution.py:23
  16.0 15.0 %copy-start.10 = (s32[3,4]{1,0:T(4,128)S(1)}, s32[3,4]{1,0:T(4,128)}, u32[]{:S(2)}) copy-start(s32[3,4]{1,0:T(4,128)} %param.9) | copy-start | bytes 148
  17.3 31.4 %collective-permute-start.1 = (bf16[2,1,384,512]{3,2,1,0:T(8,128)(2,1)}, bf16[2,1,384,512]{3,2,1,0:T(8,128)(2,1)}, u32[]{:S(2)}, u32[]{:S(2)}) collective-permute-start(bf16[2,1,384,512]{3,2,1,0:T(8,128)(2,1)} %stack.8.kn_ref.vn_ref), channel_id=1, source_target_pairs={{0,128},{2,130},{4,132},{6,134},{8,136},{10,138},{12,140},{14,142}... | collective-permute-start | bytes 2359304 | tf_op jit(solution)/shard_map/ppermute | solution.py:19
  20.5 28.2 %collective-permute-start.2 = (bf16[2,1,384,512]{3,2,1,0:T(8,128)(2,1)}, bf16[2,1,384,512]{3,2,1,0:T(8,128)(2,1)}, u32[]{:S(2)}, u32[]{:S(2)}) collective-permute-start(bf16[2,1,384,512]{3,2,1,0:T(8,128)(2,1)} %stack.8.kn_ref.vn_ref), channel_id=1, source_target_pairs={{0,64},{2,66},{4,68},{6,70},{8,72},{10,74},{12,76},{14,78},{16,80}... | collective-permute-start | bytes 2359304 | tf_op jit(solution)/shard_map/ppermute | solution.py:19
  22.6 34.7 %collective-permute-start.3 = (bf16[2,1,384,512]{3,2,1,0:T(8,128)(2,1)}, bf16[2,1,384,512]{3,2,1,0:T(8,128)(2,1)}, u32[]{:S(2)}, u32[]{:S(2)}) collective-permute-start(bf16[2,1,384,512]{3,2,1,0:T(8,128)(2,1)} %stack.8.kn_ref.vn_ref), channel_id=1, source_target_pairs={{0,32},{2,34},{4,36},{6,38},{8,40},{10,42},{12,44},{14,46},{16,48}... | collective-permute-start | bytes 2359304 | tf_op jit(solution)/shard_map/ppermute | solution.py:19
  24.1 39.5 %collective-permute-start.4 = (bf16[2,1,384,512]{3,2,1,0:T(8,128)(2,1)}, bf16[2,1,384,512]{3,2,1,0:T(8,128)(2,1)}, u32[]{:S(2)}, u32[]{:S(2)}) collective-permute-start(bf16[2,1,384,512]{3,2,1,0:T(8,128)(2,1)} %stack.8.kn_ref.vn_ref), channel_id=1, source_target_pairs={{0,16},{2,18},{4,20},{6,22},{8,24},{10,26},{12,28},{14,30},{16,0},... | collective-permute-start | bytes 2359304 | tf_op jit(solution)/shard_map/ppermute | solution.py:19
  30.4 16.0 %collective-permute-start.8 = (bf16[1,384,512]{2,1,0:T(8,128)(2,1)}, bf16[1,384,512]{2,1,0:T(8,128)(2,1)}, u32[]{:S(2)}, u32[]{:S(2)}) collective-permute-start(bf16[1,384,512]{2,1,0:T(8,128)(2,1)} %get-tuple-element.21), channel_id=1, source_target_pairs={{0,1},{1,0},{2,3},{3,2},{4,5},{5,4},{6,7},{7,6},{8,9},{9,8},{10,11... | collective-permute-start | bytes 1179656 | tf_op jit(solution)/shard_map/ppermute | solution.py:23
  46.3 44.5 %collective-permute-start.6 = (bf16[512,1024]{1,0:T(8,128)(2,1)}, bf16[512,1024]{1,0:T(8,128)(2,1)}, u32[]{:S(2)}, u32[]{:S(2)}) collective-permute-start(bf16[512,1024]{1,0:T(8,128)(2,1)} %param.11), channel_id=1, source_target_pairs={{0,129},{1,128},{2,131},{3,130},{4,133},{5,132},{6,135},{7,134},{8... | collective-permute-start | bytes 3145736 | tf_op jit(solution)/shard_map/ppermute | solution.py:35
  76.0 20.5 %collective-permute-start.5 = (bf16[1,384,512]{2,1,0:T(8,128)(2,1)}, bf16[1,384,512]{2,1,0:T(8,128)(2,1)}, u32[]{:S(2)}, u32[]{:S(2)}) collective-permute-start(bf16[1,384,512]{2,1,0:T(8,128)(2,1)} %shard_map.74), channel_id=1, source_target_pairs={{0,1},{1,0},{2,3},{3,2},{4,5},{5,4},{6,7},{7,6},{8,9},{9,8},{10,11... | collective-permute-start | bytes 1179656 | tf_op jit(solution)/shard_map/ppermute | solution.py:23
  80.2 22.3 %collective-permute-start.9 = (bf16[2,1,384,512]{3,2,1,0:T(8,128)(2,1)}, bf16[2,1,384,512]{3,2,1,0:T(8,128)(2,1)}, u32[]{:S(2)}, u32[]{:S(2)}) collective-permute-start(bf16[2,1,384,512]{3,2,1,0:T(8,128)(2,1)} %stack.9.kn_ref.vn_ref), channel_id=1, source_target_pairs={{0,128},{2,130},{4,132},{6,134},{8,136},{10,138},{12,140},{14,142}... | collective-permute-start | bytes 2359304 | tf_op jit(solution)/shard_map/ppermute | solution.py:19
  82.1 22.2 %collective-permute-start.10 = (bf16[2,1,384,512]{3,2,1,0:T(8,128)(2,1)}, bf16[2,1,384,512]{3,2,1,0:T(8,128)(2,1)}, u32[]{:S(2)}, u32[]{:S(2)}) collective-permute-start(bf16[2,1,384,512]{3,2,1,0:T(8,128)(2,1)} %stack.9.kn_ref.vn_ref), channel_id=1, source_target_pairs={{0,64},{2,66},{4,68},{6,70},{8,72},{10,74},{12,76},{14,78},{16,80}... | collective-permute-start | bytes 2359304 | tf_op jit(solution)/shard_map/ppermute | solution.py:19
  82.3 34.2 %collective-permute-start.11 = (bf16[2,1,384,512]{3,2,1,0:T(8,128)(2,1)}, bf16[2,1,384,512]{3,2,1,0:T(8,128)(2,1)}, u32[]{:S(2)}, u32[]{:S(2)}) collective-permute-start(bf16[2,1,384,512]{3,2,1,0:T(8,128)(2,1)} %stack.9.kn_ref.vn_ref), channel_id=1, source_target_pairs={{0,32},{2,34},{4,36},{6,38},{8,40},{10,42},{12,44},{14,46},{16,48}... | collective-permute-start | bytes 2359304 | tf_op jit(solution)/shard_map/ppermute | solution.py:19
  90.9 33.9 %collective-permute-start.12 = (bf16[2,1,384,512]{3,2,1,0:T(8,128)(2,1)}, bf16[2,1,384,512]{3,2,1,0:T(8,128)(2,1)}, u32[]{:S(2)}, u32[]{:S(2)}) collective-permute-start(bf16[2,1,384,512]{3,2,1,0:T(8,128)(2,1)} %stack.9.kn_ref.vn_ref), channel_id=1, source_target_pairs={{0,16},{2,18},{4,20},{6,22},{8,24},{10,26},{12,28},{14,30},{16,0},... | collective-permute-start | bytes 2359304 | tf_op jit(solution)/shard_map/ppermute | solution.py:19
  137.1 12.3 %collective-permute-start.13 = (bf16[1,384,512]{2,1,0:T(8,128)(2,1)}, bf16[1,384,512]{2,1,0:T(8,128)(2,1)S(1)}, u32[]{:S(2)}, u32[]{:S(2)}) collective-permute-start(bf16[1,384,512]{2,1,0:T(8,128)(2,1)} %shard_map.76), channel_id=1, source_target_pairs={{0,1},{1,0},{2,3},{3,2},{4,5},{5,4},{6,7},{7,6},{8,9},{9,8},{10,11... | collective-permute-start | bytes 1179656 | tf_op jit(solution)/shard_map/ppermute | solution.py:23
  142.8 8.4 %copy-start.4 = (bf16[1,384,512]{2,1,0:T(8,128)(2,1)S(1)}, bf16[1,384,512]{2,1,0:T(8,128)(2,1)}, u32[]{:S(2)}) copy-start(bf16[1,384,512]{2,1,0:T(8,128)(2,1)} %copy-done.3) | copy-start | bytes 1179652
  142.8 8.4 %copy-start.6 = (bf16[1,384,512]{2,1,0:T(8,128)(2,1)S(1)}, bf16[1,384,512]{2,1,0:T(8,128)(2,1)}, u32[]{:S(2)}) copy-start(bf16[1,384,512]{2,1,0:T(8,128)(2,1)} %copy-done.5) | copy-start | bytes 1179652
  142.8 8.4 %copy-start.9 = (bf16[1,384,512]{2,1,0:T(8,128)(2,1)S(1)}, bf16[1,384,512]{2,1,0:T(8,128)(2,1)}, u32[]{:S(2)}) copy-start(bf16[1,384,512]{2,1,0:T(8,128)(2,1)} %shard_map.76) | copy-start | bytes 1179652
  142.8 8.4 %copy-start.15 = (bf16[512,1024]{1,0:T(8,128)(2,1)S(1)}, bf16[512,1024]{1,0:T(8,128)(2,1)}, u32[]{:S(2)}) copy-start(bf16[512,1024]{1,0:T(8,128)(2,1)} %param.11) | copy-start | bytes 3145732
  142.8 14.0 %collective-permute-start.7 = (bf16[1,384,512]{2,1,0:T(8,128)(2,1)}, bf16[1,384,512]{2,1,0:T(8,128)(2,1)S(1)}, u32[]{:S(2)}, u32[]{:S(2)}) collective-permute-start(bf16[1,384,512]{2,1,0:T(8,128)(2,1)} %fusion.51), channel_id=1, source_target_pairs={{0,1},{1,0},{2,3},{3,2},{4,5},{5,4},{6,7},{7,6},{8,9},{9,8},{10,11... | collective-permute-start | bytes 1179656 | tf_op jit(solution)/shard_map/ppermute | solution.py:23
  156.7 9.5 %collective-permute-start.14 = (bf16[1,384,512]{2,1,0:T(8,128)(2,1)}, bf16[1,384,512]{2,1,0:T(8,128)(2,1)}, u32[]{:S(2)}, u32[]{:S(2)}) collective-permute-start(bf16[1,384,512]{2,1,0:T(8,128)(2,1)} %fusion.48), channel_id=1, source_target_pairs={{0,1},{1,0},{2,3},{3,2},{4,5},{5,4},{6,7},{7,6},{8,9},{9,8},{10,11... | collective-permute-start | bytes 1179656 | tf_op jit(solution)/shard_map/ppermute | solution.py:23
  156.7 9.5 %copy-start.13 = (bf16[1536,1024]{1,0:T(8,128)(2,1)S(1)}, bf16[1536,1024]{1,0:T(8,128)(2,1)}, u32[]{:S(2)}) copy-start(bf16[1536,1024]{1,0:T(8,128)(2,1)} %param.13) | copy-start | bytes 9437188
  156.7 9.5 %copy-start.17 = (bf16[384,1024]{1,0:T(8,128)(2,1)S(1)}, bf16[384,1024]{1,0:T(8,128)(2,1)}, u32[]{:S(2)}) copy-start(bf16[384,1024]{1,0:T(8,128)(2,1)} %copy-done.16) | copy-start | bytes 2359300
  156.7 9.5 %copy-start.20 = (bf16[384,1536]{1,0:T(8,128)(2,1)S(1)}, bf16[384,1536]{1,0:T(8,128)(2,1)}, u32[]{:S(2)}) copy-start(bf16[384,1536]{1,0:T(8,128)(2,1)} %copy-done.19) | copy-start | bytes 3538948
  (12 other events, 39.7 us)

commit v3 on v2

--- a/solution.py
+++ b/solution.py
@@ -33,12 +33,6 @@
         for t in range(tp_size)
     ]
     return lax.ppermute(w_out, ("seq", "tp"), perm)
-
-
-def tp_join(own, other, tp_index):
-    first = jnp.where(tp_index == 0, own, other)
-    second = jnp.where(tp_index == 0, other, own)
-    return jnp.concatenate([first, second], axis=-1)
 
 
 def tp_half(x, index, width):
@@ -202,7 +196,9 @@
     samples, tok_rows, half_width = noisy.shape
     tp_index = lax.axis_index("tp")
     noisy_other = tp_swap(noisy)
-    gathered = tp_join(noisy, noisy_other, tp_index)
+    gathered = lax.dynamic_update_slice_in_dim(
+        jnp.concatenate([noisy_other, noisy_other], axis=-1), noisy, tp_index * half_width, axis=2
+    )
     normed = condition(gathered, level_feat)
     projected = jnp.einsum(
         "std,cde->cste", normed, w_qkv, preferred_element_type=jnp.float32

time: 170 us -> 166 us (0.976)
  matrix products: 23.6 us -> 19 us
  starting transfers between devices: 28.5 us -> 31.2 us
    ppermute x6, waiting for transfers between devices: 27.3 us -> 20.5 us  [tp_swap(): return lax.ppermute(x, 'tp', [(0, 1), (1, 0)])]
    ppermute x8, waiting for transfers between devices: 39.6 us -> 45.3 us  [partner(): lax.ppermute(x, axis, [(i, i ^ 1 << stride) for i in range(lax.axis_size(...]
    select_n x2 -> x0, other arithmetic: 3.24 us -> none  [tp_join(): first = jnp.where(tp_index == 0, own, other)]
    dot_general x2, matrix products: 4.56 us -> 1.64 us  [one_sample(): jnp.einsum('stf,fd->std', hidden, w_down_own, preferred_element_type=jnp....]
    concatenate x0 -> x2, other arithmetic: none -> 2.37 us  [one_sample(): jnp.concatenate([noisy_other, noisy_other], axis=-1)]
  transfers between devices with their start and end apart: 15 -> 15, of which waited for: 11 -> 10; matrix products, arithmetic and copies ran while one was open for 16% -> 16% of each run, Pallas kernels for 14% -> 14%
where the time goes in v3:
time: 166 us; the launch traced here: 165 us
  waiting for transfers between devices  65.8 us (40%)
  Pallas kernels  35.5 us (21%)
  starting transfers between devices  31.2 us (19%)
  matrix products  19 us (11%)
  local copies, waits for them, and re-layouts  8.41 us (5%)
  other arithmetic  5.33 us (3%)
    ppermute x8, waiting for transfers between devices, partner(): lax.ppermute(x, axis, [(i, i ^ 1 << stride) for i in range(lax.axis_size(...  45.3 us
    pallas_call x2, Pallas kernels, far_attention(): pl.pallas_call(functools.partial(far_kernel, head_dim=head_dim), grid_spe...  24.8 us
    ppermute x8, starting transfers between devices, partner(): lax.ppermute(x, axis, [(i, i ^ 1 << stride) for i in range(lax.axis_size(...  24.1 us
    ppermute x6, waiting for transfers between devices, tp_swap(): return lax.ppermute(x, 'tp', [(0, 1), (1, 0)])  20.5 us
    pallas_call x2, Pallas kernels, near_attention(): pl.pallas_call(functools.partial(near_kernel, head_dim=head_dim), grid=(w...  10.7 us
    ppermute x6, starting transfers between devices, tp_swap(): return lax.ppermute(x, 'tp', [(0, 1), (1, 0)])  6.81 us
    dot_general x2, matrix products, one_sample(): jnp.einsum('std,df->stf', inner, w_up, preferred_element_type=jnp.float32)  5.74 us
    dot_general x2, matrix products, one_sample(): jnp.einsum('std,cde->cste', normed, w_qkv, preferred_element_type=jnp.flo...  4.05 us
  transfers between devices with their start and end apart: 15, of which 10 were waited for; matrix products, arithmetic and copies ran while one was open for 16% of the time, Pallas kernels for 14%

profile of v3, /device:TPU:34, one launch (start us, length us, event | category | flops | bytes accessed | tf_op | source)
XLA Modules:
  0.0 165.5 jit_solution(2901349067749040021)
XLA Ops:
  5.0 7.2 %collective-permute-done = bf16[1,384,512]{2,1,0:T(8,128)(2,1)} collective-permute-done((bf16[1,384,512]{2,1,0:T(8,128)(2,1)S(1)}, bf16[1,384,512]{2,1,0:T(8,128)(2,1)}, u32[]{:S(2)}, u32[]{:S(2)}) %collective-permute-start) | collective-permute-done | bytes 393248 | tf_op jit(solution)/shard_map/ppermute | solution.py:23
  17.8 2.1 %collective-permute-start.2 = (bf16[2,1,384,512]{3,2,1,0:T(8,128)(2,1)}, bf16[2,1,384,512]{3,2,1,0:T(8,128)(2,1)}, u32[]{:S(2)}, u32[]{:S(2)}) collective-permute-start(bf16[2,1,384,512]{3,2,1,0:T(8,128)(2,1)} %stack.8.kn_ref.vn_ref), channel_id=1, source_target_pairs={{0,64},{2,66},{4,68},{6,70},{8,72},{10,74},{12,76},{14,78},{16,80}... | collective-permute-start | bytes 2359304 | tf_op jit(solution)/shard_map/ppermute | solution.py:19
  21.4 6.3 %collective-permute-start.4 = (bf16[2,1,384,512]{3,2,1,0:T(8,128)(2,1)}, bf16[2,1,384,512]{3,2,1,0:T(8,128)(2,1)}, u32[]{:S(2)}, u32[]{:S(2)}) collective-permute-start(bf16[2,1,384,512]{3,2,1,0:T(8,128)(2,1)} %stack.8.kn_ref.vn_ref), channel_id=1, source_target_pairs={{0,16},{2,18},{4,20},{6,22},{8,24},{10,26},{12,28},{14,30},{16,0},... | collective-permute-start | bytes 2359304 | tf_op jit(solution)/shard_map/ppermute | solution.py:19
  27.7 2.9 %collective-permute-start.1 = (bf16[2,1,384,512]{3,2,1,0:T(8,128)(2,1)}, bf16[2,1,384,512]{3,2,1,0:T(8,128)(2,1)}, u32[]{:S(2)}, u32[]{:S(2)}) collective-permute-start(bf16[2,1,384,512]{3,2,1,0:T(8,128)(2,1)} %stack.8.kn_ref.vn_ref), channel_id=1, source_target_pairs={{0,128},{2,130},{4,132},{6,134},{8,136},{10,138},{12,140},{14,142}... | collective-permute-start | bytes 2359304 | tf_op jit(solution)/shard_map/ppermute | solution.py:19
  31.4 5.4 %shard_map.73 = (bf16[1,384,512]{2,1,0:T(8,128)(2,1)}, f32[1,384,512]{2,1,0:T(8,128)}, f32[1,384,512]{2,1,0:T(8,128)}) custom-call(bf16[1,384,512]{2,1,0:T(8,128)(2,1)} %slice_bitcast_fusion.1.q_ref, bf16[2,1,384,512]{3,2,1,0:T(8,128)(2,1)} %stack.8.kn_ref.vn_ref, bf16[2,1,384,512]{3,2,1,0:T(8,128)(2,1)} %stack.8.kn_ref.vn_ref), custom_call_target="tpu_custom_call" | custom-call | tf_op jit(solution)/shard_map/pallas_call | solution.py:120
  40.4 14.2 %collective-permute-done.3 = bf16[2,1,384,512]{3,2,1,0:T(8,128)(2,1)} collective-permute-done((bf16[2,1,384,512]{3,2,1,0:T(8,128)(2,1)}, bf16[2,1,384,512]{3,2,1,0:T(8,128)(2,1)}, u32[]{:S(2)}, u32[]{:S(2)}) %collective-permute-start.3) | collective-permute-done | bytes 786464 | tf_op jit(solution)/shard_map/ppermute | solution.py:19
  54.7 6.2 %collective-permute-done.4 = bf16[2,1,384,512]{3,2,1,0:T(8,128)(2,1)} collective-permute-done((bf16[2,1,384,512]{3,2,1,0:T(8,128)(2,1)}, bf16[2,1,384,512]{3,2,1,0:T(8,128)(2,1)}, u32[]{:S(2)}, u32[]{:S(2)}) %collective-permute-start.4) | collective-permute-done | bytes 786464 | tf_op jit(solution)/shard_map/ppermute | solution.py:19
  60.9 12.4 %shard_map.74 = bf16[1,384,512]{2,1,0:T(8,128)(2,1)} custom-call(s32[12]{0:T(128)} %reshape.162.off_ref, bf16[1,384,512]{2,1,0:T(8,128)(2,1)} %slice_bitcast_fusion.1.q_ref, bf16[1,384,512]{2,1,0:T(8,128)(2,1)} %get-tuple-element.11.on_ref, f32[1,384,512]{2,1,0:T(8,128)} %get-tuple-element.12.mn_ref, f32[1,384,512]{2,1,0:T(8,128)} %get-tuple-element.13.ln_ref, ...), custom_call_target="tpu_custom_call" | custom-call | tf_op jit(solution)/shard_map/pallas_call | solution.py:155
  73.8 2.6 %fusion.29 = bf16[3,1,384,512]{3,2,1,0:T(8,128)(2,1)S(1)} fusion(bf16[3,1024,512]{2,1,0:T(8,128)(2,1)S(1)} %copy-done, bf16[1,384,1024]{2,1,0:T(8,128)(2,1)} %copy-done.3, f32[1024]{0:T(1024)S(1)} %bitcast.88, f32[384]{0:T(512)S(1)} %add_rsqrt_fusion.1), kind=kOutput, calls=%fused_computation.43 | convolution fusion | flops 1210122240 | bytes 5117440 | tf_op jit(solution)/shard_map/std,cde->cste/dot_general | solution.py:203
  77.3 3.2 %collective-permute-start.9 = (bf16[2,1,384,512]{3,2,1,0:T(8,128)(2,1)}, bf16[2,1,384,512]{3,2,1,0:T(8,128)(2,1)}, u32[]{:S(2)}, u32[]{:S(2)}) collective-permute-start(bf16[2,1,384,512]{3,2,1,0:T(8,128)(2,1)} %stack.9.kn_ref.vn_ref), channel_id=1, source_target_pairs={{0,128},{2,130},{4,132},{6,134},{8,136},{10,138},{12,140},{14,142}... | collective-permute-start | bytes 2359304 | tf_op jit(solution)/shard_map/ppermute | solution.py:19
  80.8 2.3 %collective-permute-start.11 = (bf16[2,1,384,512]{3,2,1,0:T(8,128)(2,1)}, bf16[2,1,384,512]{3,2,1,0:T(8,128)(2,1)}, u32[]{:S(2)}, u32[]{:S(2)}) collective-permute-start(bf16[2,1,384,512]{3,2,1,0:T(8,128)(2,1)} %stack.9.kn_ref.vn_ref), channel_id=1, source_target_pairs={{0,32},{2,34},{4,36},{6,38},{8,40},{10,42},{12,44},{14,46},{16,48}... | collective-permute-start | bytes 2359304 | tf_op jit(solution)/shard_map/ppermute | solution.py:19
  83.9 5.3 %shard_map.75 = (bf16[1,384,512]{2,1,0:T(8,128)(2,1)}, f32[1,384,512]{2,1,0:T(8,128)}, f32[1,384,512]{2,1,0:T(8,128)}) custom-call(bf16[1,384,512]{2,1,0:T(8,128)(2,1)} %slice_bitcast_fusion.q_ref, bf16[2,1,384,512]{3,2,1,0:T(8,128)(2,1)} %stack.9.kn_ref.vn_ref, bf16[2,1,384,512]{3,2,1,0:T(8,128)(2,1)} %stack.9.kn_ref.vn_ref), custom_call_target="tpu_custom_call" | custom-call | tf_op jit(solution)/shard_map/pallas_call | solution.py:120
  89.3 5.5 %collective-permute-start.12 = (bf16[2,1,384,512]{3,2,1,0:T(8,128)(2,1)}, bf16[2,1,384,512]{3,2,1,0:T(8,128)(2,1)}, u32[]{:S(2)}, u32[]{:S(2)}) collective-permute-start(bf16[2,1,384,512]{3,2,1,0:T(8,128)(2,1)} %stack.9.kn_ref.vn_ref), channel_id=1, source_target_pairs={{0,16},{2,18},{4,20},{6,22},{8,24},{10,26},{12,28},{14,30},{16,0},... | collective-permute-start | bytes 2359304 | tf_op jit(solution)/shard_map/ppermute | solution.py:19
  94.8 1.8 %fusion.79 = f32[384,1024]{1,0:T(8,128)S(1)} fusion(bf16[512,1024]{1,0:T(8,128)(2,1)} %collective-permute-done.6, bf16[1,384,512]{2,1,0:T(8,128)(2,1)S(1)} %collective-permute-done.5), kind=kOutput, calls=%fused_computation.80 | convolution fusion | flops 402653184 | bytes 3014656 | tf_op jit(solution)/shard_map/sth,hd->std/dot_general | solution.py:223
  98.2 2.7 %collective-permute-done.9 = bf16[2,1,384,512]{3,2,1,0:T(8,128)(2,1)} collective-permute-done((bf16[2,1,384,512]{3,2,1,0:T(8,128)(2,1)}, bf16[2,1,384,512]{3,2,1,0:T(8,128)(2,1)}, u32[]{:S(2)}, u32[]{:S(2)}) %collective-permute-start.9) | collective-permute-done | bytes 786464 | tf_op jit(solution)/shard_map/ppermute | solution.py:19
  100.9 1.8 %collective-permute-done.10 = bf16[2,1,384,512]{3,2,1,0:T(8,128)(2,1)} collective-permute-done((bf16[2,1,384,512]{3,2,1,0:T(8,128)(2,1)}, bf16[2,1,384,512]{3,2,1,0:T(8,128)(2,1)}, u32[]{:S(2)}, u32[]{:S(2)}) %collective-permute-start.10) | collective-permute-done | bytes 786464 | tf_op jit(solution)/shard_map/ppermute | solution.py:19
  102.7 12.2 %collective-permute-done.11 = bf16[2,1,384,512]{3,2,1,0:T(8,128)(2,1)} collective-permute-done((bf16[2,1,384,512]{3,2,1,0:T(8,128)(2,1)}, bf16[2,1,384,512]{3,2,1,0:T(8,128)(2,1)}, u32[]{:S(2)}, u32[]{:S(2)}) %collective-permute-start.11) | collective-permute-done | bytes 786464 | tf_op jit(solution)/shard_map/ppermute | solution.py:19
  114.9 8.2 %collective-permute-done.12 = bf16[2,1,384,512]{3,2,1,0:T(8,128)(2,1)} collective-permute-done((bf16[2,1,384,512]{3,2,1,0:T(8,128)(2,1)}, bf16[2,1,384,512]{3,2,1,0:T(8,128)(2,1)}, u32[]{:S(2)}, u32[]{:S(2)}) %collective-permute-start.12) | collective-permute-done | bytes 786464 | tf_op jit(solution)/shard_map/ppermute | solution.py:19
  123.1 12.4 %shard_map.76 = bf16[1,384,512]{2,1,0:T(8,128)(2,1)} custom-call(s32[12]{0:T(128)} %reshape.162.off_ref, bf16[1,384,512]{2,1,0:T(8,128)(2,1)} %slice_bitcast_fusion.q_ref, bf16[1,384,512]{2,1,0:T(8,128)(2,1)} %get-tuple-element.14.on_ref, f32[1,384,512]{2,1,0:T(8,128)} %get-tuple-element.15.mn_ref, f32[1,384,512]{2,1,0:T(8,128)} %get-tuple-element.16.ln_ref, ...), custom_call_target="tpu_custom_call" | custom-call | tf_op jit(solution)/shard_map/pallas_call | solution.py:155
  136.3 4.0 %fusion.7 = bf16[384,1536]{1,0:T(8,128)(2,1)S(1)} fusion(bf16[1024,1536]{1,0:T(8,128)(2,1)} %param.12, bf16[1,384,1024]{2,1,0:T(8,128)(2,1)} %get-tuple-element.26, f32[384]{0:T(512)S(1)} %add_rsqrt_fusion.2), kind=kOutput, calls=%fused_computation.15 | convolution fusion | flops 1214447616 | bytes 5113344 | tf_op jit(solution)/shard_map/std,df->stf/dot_general | solution.py:230
  142.6 5.2 %collective-permute-done.13 = bf16[1,384,512]{2,1,0:T(8,128)(2,1)S(1)} collective-permute-done((bf16[1,384,512]{2,1,0:T(8,128)(2,1)}, bf16[1,384,512]{2,1,0:T(8,128)(2,1)S(1)}, u32[]{:S(2)}, u32[]{:S(2)}) %collective-permute-start.13) | collective-permute-done | bytes 393248 | tf_op jit(solution)/shard_map/ppermute | solution.py:23
  147.8 1.8 %fusion.76 = f32[384,1024]{1,0:T(8,128)S(1)} fusion(bf16[512,1024]{1,0:T(8,128)(2,1)} %collective-permute-done.6, bf16[1,384,512]{2,1,0:T(8,128)(2,1)S(1)} %collective-permute-done.13), kind=kOutput, calls=%fused_computation.77 | convolution fusion | flops 402653184 | bytes 3014656 | tf_op jit(solution)/shard_map/sth,hd->std/dot_general | solution.py:223
  151.5 1.7 %fusion.15 = bf16[384,1536]{1,0:T(8,128)(2,1)S(1)} fusion(bf16[1024,1536]{1,0:T(8,128)(2,1)S(1)} %copy-done.11, bf16[1,384,1024]{2,1,0:T(8,128)(2,1)S(1)} %get-tuple-element.24, f32[384]{0:T(512)S(1)} %add_rsqrt_fusion), kind=kOutput, calls=%fused_computation.23 | convolution fusion | flops 1214447616 | bytes 5113344 | tf_op jit(solution)/shard_map/std,df->stf/dot_general | solution.py:230
  156.3 7.4 %collective-permute-done.14 = bf16[1,384,512]{2,1,0:T(8,128)(2,1)S(1)} collective-permute-done((bf16[1,384,512]{2,1,0:T(8,128)(2,1)S(1)}, bf16[1,384,512]{2,1,0:T(8,128)(2,1)S(1)}, u32[]{:S(2)}, u32[]{:S(2)}) %collective-permute-start.14) | collective-permute-done | bytes 393248 | tf_op jit(solution)/shard_map/ppermute | solution.py:23
  (70 shorter events, 30.3 us)
Async XLA Ops:
  0.0 15.4 %copy-start = (bf16[3,1024,512]{2,1,0:T(8,128)(2,1)S(1)}, bf16[3,1024,512]{2,1,0:T(8,128)(2,1)}, u32[]{:S(2)}) copy-start(bf16[3,1024,512]{2,1,0:T(8,128)(2,1)} %param.10) | copy-start | bytes 9437188
  1.2 11.0 %collective-permute-start = (bf16[1,384,512]{2,1,0:T(8,128)(2,1)S(1)}, bf16[1,384,512]{2,1,0:T(8,128)(2,1)}, u32[]{:S(2)}, u32[]{:S(2)}) collective-permute-start(bf16[1,384,512]{2,1,0:T(8,128)(2,1)S(1)} %slice.24), channel_id=1, source_target_pairs={{0,1},{1,0},{2,3},{3,2},{4,5},{5,4},{6,7},{7,6},{8,9},{9,8},{10,11... | collective-permute-start | bytes 1179656 | tf_op jit(solution)/shard_map/ppermute | solution.py:23
  4.8 8.6 %copy-start.7 = (bf16[2,384,512]{2,1,0:T(8,128)(2,1)S(1)}, bf16[2,384,512]{2,1,0:T(8,128)(2,1)}, u32[]{:S(2)}) copy-start(bf16[2,384,512]{2,1,0:T(8,128)(2,1)} %param.7) | copy-start | bytes 2359300
  13.7 23.0 %collective-permute-start.8 = (bf16[1,384,512]{2,1,0:T(8,128)(2,1)S(1)}, bf16[1,384,512]{2,1,0:T(8,128)(2,1)}, u32[]{:S(2)}, u32[]{:S(2)}) collective-permute-start(bf16[1,384,512]{2,1,0:T(8,128)(2,1)S(1)} %get-tuple-element.18), channel_id=1, source_target_pairs={{0,1},{1,0},{2,3},{3,2},{4,5},{5,4},{6,7},{7,6},{8,9},{9,8},{10,11... | collective-permute-start | bytes 1179656 | tf_op jit(solution)/shard_map/ppermute | solution.py:23
  17.8 22.6 %collective-permute-start.2 = (bf16[2,1,384,512]{3,2,1,0:T(8,128)(2,1)}, bf16[2,1,384,512]{3,2,1,0:T(8,128)(2,1)}, u32[]{:S(2)}, u32[]{:S(2)}) collective-permute-start(bf16[2,1,384,512]{3,2,1,0:T(8,128)(2,1)} %stack.8.kn_ref.vn_ref), channel_id=1, source_target_pairs={{0,64},{2,66},{4,68},{6,70},{8,72},{10,74},{12,76},{14,78},{16,80}... | collective-permute-start | bytes 2359304 | tf_op jit(solution)/shard_map/ppermute | solution.py:19
  19.9 34.7 %collective-permute-start.3 = (bf16[2,1,384,512]{3,2,1,0:T(8,128)(2,1)}, bf16[2,1,384,512]{3,2,1,0:T(8,128)(2,1)}, u32[]{:S(2)}, u32[]{:S(2)}) collective-permute-start(bf16[2,1,384,512]{3,2,1,0:T(8,128)(2,1)} %stack.8.kn_ref.vn_ref), channel_id=1, source_target_pairs={{0,32},{2,34},{4,36},{6,38},{8,40},{10,42},{12,44},{14,46},{16,48}... | collective-permute-start | bytes 2359304 | tf_op jit(solution)/shard_map/ppermute | solution.py:19
  21.4 39.5 %collective-permute-start.4 = (bf16[2,1,384,512]{3,2,1,0:T(8,128)(2,1)}, bf16[2,1,384,512]{3,2,1,0:T(8,128)(2,1)}, u32[]{:S(2)}, u32[]{:S(2)}) collective-permute-start(bf16[2,1,384,512]{3,2,1,0:T(8,128)(2,1)} %stack.8.kn_ref.vn_ref), channel_id=1, source_target_pairs={{0,16},{2,18},{4,20},{6,22},{8,24},{10,26},{12,28},{14,30},{16,0},... | collective-permute-start | bytes 2359304 | tf_op jit(solution)/shard_map/ppermute | solution.py:19
  27.7 33.2 %collective-permute-start.1 = (bf16[2,1,384,512]{3,2,1,0:T(8,128)(2,1)}, bf16[2,1,384,512]{3,2,1,0:T(8,128)(2,1)}, u32[]{:S(2)}, u32[]{:S(2)}) collective-permute-start(bf16[2,1,384,512]{3,2,1,0:T(8,128)(2,1)} %stack.8.kn_ref.vn_ref), channel_id=1, source_target_pairs={{0,128},{2,130},{4,132},{6,134},{8,136},{10,138},{12,140},{14,142}... | collective-permute-start | bytes 2359304 | tf_op jit(solution)/shard_map/ppermute | solution.py:19
  36.7 52.5 %collective-permute-start.6 = (bf16[512,1024]{1,0:T(8,128)(2,1)}, bf16[512,1024]{1,0:T(8,128)(2,1)}, u32[]{:S(2)}, u32[]{:S(2)}) collective-permute-start(bf16[512,1024]{1,0:T(8,128)(2,1)} %param.11), channel_id=1, source_target_pairs={{0,129},{1,128},{2,131},{3,130},{4,133},{5,132},{6,135},{7,134},{8... | collective-permute-start | bytes 3145736 | tf_op jit(solution)/shard_map/ppermute | solution.py:35
  73.2 21.6 %collective-permute-start.5 = (bf16[1,384,512]{2,1,0:T(8,128)(2,1)}, bf16[1,384,512]{2,1,0:T(8,128)(2,1)S(1)}, u32[]{:S(2)}, u32[]{:S(2)}) collective-permute-start(bf16[1,384,512]{2,1,0:T(8,128)(2,1)} %shard_map.74), channel_id=1, source_target_pairs={{0,1},{1,0},{2,3},{3,2},{4,5},{5,4},{6,7},{7,6},{8,9},{9,8},{10,11... | collective-permute-start | bytes 1179656 | tf_op jit(solution)/shard_map/ppermute | solution.py:23
  77.3 23.7 %collective-permute-start.9 = (bf16[2,1,384,512]{3,2,1,0:T(8,128)(2,1)}, bf16[2,1,384,512]{3,2,1,0:T(8,128)(2,1)}, u32[]{:S(2)}, u32[]{:S(2)}) collective-permute-start(bf16[2,1,384,512]{3,2,1,0:T(8,128)(2,1)} %stack.9.kn_ref.vn_ref), channel_id=1, source_target_pairs={{0,128},{2,130},{4,132},{6,134},{8,136},{10,138},{12,140},{14,142}... | collective-permute-start | bytes 2359304 | tf_op jit(solution)/shard_map/ppermute | solution.py:19
  80.5 22.2 %collective-permute-start.10 = (bf16[2,1,384,512]{3,2,1,0:T(8,128)(2,1)}, bf16[2,1,384,512]{3,2,1,0:T(8,128)(2,1)}, u32[]{:S(2)}, u32[]{:S(2)}) collective-permute-start(bf16[2,1,384,512]{3,2,1,0:T(8,128)(2,1)} %stack.9.kn_ref.vn_ref), channel_id=1, source_target_pairs={{0,64},{2,66},{4,68},{6,70},{8,72},{10,74},{12,76},{14,78},{16,80}... | collective-permute-start | bytes 2359304 | tf_op jit(solution)/shard_map/ppermute | solution.py:19
  80.8 34.2 %collective-permute-start.11 = (bf16[2,1,384,512]{3,2,1,0:T(8,128)(2,1)}, bf16[2,1,384,512]{3,2,1,0:T(8,128)(2,1)}, u32[]{:S(2)}, u32[]{:S(2)}) collective-permute-start(bf16[2,1,384,512]{3,2,1,0:T(8,128)(2,1)} %stack.9.kn_ref.vn_ref), channel_id=1, source_target_pairs={{0,32},{2,34},{4,36},{6,38},{8,40},{10,42},{12,44},{14,46},{16,48}... | collective-permute-start | bytes 2359304 | tf_op jit(solution)/shard_map/ppermute | solution.py:19
  89.2 7.4 %copy-start.2 = (bf16[1,384,1024]{2,1,0:T(8,128)(2,1)S(1)}, bf16[1,384,1024]{2,1,0:T(8,128)(2,1)}, u32[]{:S(2)}) copy-start(bf16[1,384,1024]{2,1,0:T(8,128)(2,1)} %copy-done.1) | copy-start | bytes 2359300
  89.2 7.4 %copy-start.5 = (bf16[512,1024]{1,0:T(8,128)(2,1)S(1)}, bf16[512,1024]{1,0:T(8,128)(2,1)}, u32[]{:S(2)}) copy-start(bf16[512,1024]{1,0:T(8,128)(2,1)} %param.11) | copy-start | bytes 3145732
  89.2 7.4 %copy-start.8 = (bf16[1,384,512]{2,1,0:T(8,128)(2,1)S(1)}, bf16[1,384,512]{2,1,0:T(8,128)(2,1)}, u32[]{:S(2)}) copy-start(bf16[1,384,512]{2,1,0:T(8,128)(2,1)} %shard_map.74) | copy-start | bytes 1179652
  89.3 33.9 %collective-permute-start.12 = (bf16[2,1,384,512]{3,2,1,0:T(8,128)(2,1)}, bf16[2,1,384,512]{3,2,1,0:T(8,128)(2,1)}, u32[]{:S(2)}, u32[]{:S(2)}) collective-permute-start(bf16[2,1,384,512]{3,2,1,0:T(8,128)(2,1)} %stack.9.kn_ref.vn_ref), channel_id=1, source_target_pairs={{0,16},{2,18},{4,20},{6,22},{8,24},{10,26},{12,28},{14,30},{16,0},... | collective-permute-start | bytes 2359304 | tf_op jit(solution)/shard_map/ppermute | solution.py:19
  135.5 12.3 %collective-permute-start.13 = (bf16[1,384,512]{2,1,0:T(8,128)(2,1)}, bf16[1,384,512]{2,1,0:T(8,128)(2,1)S(1)}, u32[]{:S(2)}, u32[]{:S(2)}) collective-permute-start(bf16[1,384,512]{2,1,0:T(8,128)(2,1)} %shard_map.76), channel_id=1, source_target_pairs={{0,1},{1,0},{2,3},{3,2},{4,5},{5,4},{6,7},{7,6},{8,9},{9,8},{10,11... | collective-permute-start | bytes 1179656 | tf_op jit(solution)/shard_map/ppermute | solution.py:23
  136.3 4.0 %copy-start.12 = (bf16[1536,1024]{1,0:T(8,128)(2,1)S(1)}, bf16[1536,1024]{1,0:T(8,128)(2,1)}, u32[]{:S(2)}) copy-start(bf16[1536,1024]{1,0:T(8,128)(2,1)} %param.13) | copy-start | bytes 9437188
  141.1 8.5 %copy-start.4 = (bf16[1,384,1024]{2,1,0:T(8,128)(2,1)S(1)}, bf16[1,384,1024]{2,1,0:T(8,128)(2,1)}, u32[]{:S(2)}) copy-start(bf16[1,384,1024]{2,1,0:T(8,128)(2,1)} %copy-done.3) | copy-start | bytes 2359300
  141.1 8.5 %copy-start.6 = (bf16[512,1024]{1,0:T(8,128)(2,1)S(1)}, bf16[512,1024]{1,0:T(8,128)(2,1)}, u32[]{:S(2)}) copy-start(bf16[512,1024]{1,0:T(8,128)(2,1)} %param.11) | copy-start | bytes 3145732
  141.1 8.5 %copy-start.9 = (bf16[1,384,512]{2,1,0:T(8,128)(2,1)S(1)}, bf16[1,384,512]{2,1,0:T(8,128)(2,1)}, u32[]{:S(2)}) copy-start(bf16[1,384,512]{2,1,0:T(8,128)(2,1)} %shard_map.76) | copy-start | bytes 1179652
  141.1 14.4 %collective-permute-start.7 = (bf16[1,384,512]{2,1,0:T(8,128)(2,1)S(1)}, bf16[1,384,512]{2,1,0:T(8,128)(2,1)S(1)}, u32[]{:S(2)}, u32[]{:S(2)}) collective-permute-start(bf16[1,384,512]{2,1,0:T(8,128)(2,1)S(1)} %fusion.53), channel_id=1, source_target_pairs={{0,1},{1,0},{2,3},{3,2},{4,5},{5,4},{6,7},{7,6},{8,9},{9,8},{10,11... | collective-permute-start | bytes 1179656 | tf_op jit(solution)/shard_map/ppermute | solution.py:23
  154.1 9.6 %collective-permute-start.14 = (bf16[1,384,512]{2,1,0:T(8,128)(2,1)S(1)}, bf16[1,384,512]{2,1,0:T(8,128)(2,1)S(1)}, u32[]{:S(2)}, u32[]{:S(2)}) collective-permute-start(bf16[1,384,512]{2,1,0:T(8,128)(2,1)S(1)} %fusion.50), channel_id=1, source_target_pairs={{0,1},{1,0},{2,3},{3,2},{4,5},{5,4},{6,7},{7,6},{8,9},{9,8},{10,11... | collective-permute-start | bytes 1179656 | tf_op jit(solution)/shard_map/ppermute | solution.py:23
  (4 other events, 8.4 us)
